TPU v7x, 32 devices: a whole 2x2x4 slice. The times are simulated.
32 devices in a mesh: real: 2 (over x), los: 8 (over z, y), sky: 2 (over core).
Axes of the slice: x: 2, y: 2, z: 4, core: 2. Of those that a mesh axis runs over, the one named last changes fastest.
Arguments:
- density: float32 [16, 2048, 2048], P(('real', 'los'), 'sky'), parts along dimension 0, may hold values from -6 to 8
- lens_weight: float32 [16], P(('real', 'los')), parts along dimension 0, may hold values from 0.05 to 0.4
- plane_count: int32 [16], P(('real', 'los')), parts along dimension 0, may hold values from 0 to 1
- ray_state: float32 [16, 12, 32, 2048], P(('real', 'los'), None, 'sky'), parts along dimension 0, may hold values from -6 to 6
Outputs:
- ray_out: float32 [16, 12, 32, 2048], P(('real', 'los'), None, 'sky'), parts along dimension 0
There are 2 independent parts, one for each index of `real`. A program takes and returns all parts, laid end to end along the dimension named above; each array names one. Nothing has to cross between parts.
All inputs are finite; a program needn't handle non-finite values.
Results may differ from a plain program's by a relative error of at most 0.00012.
Values sent between devices are 32-bit elements; how exact they have to be, the bound alone decides.
No kernel may reach another device: no remote copies, remote signals or barrier semaphores. Data moves between devices by JAX's collectives and lax.ppermute only.
A program may use at most 128 MiB of HBM per device.

v0:
```python
import math

import jax
import jax.numpy as jnp
from jax import lax
from jax.sharding import PartitionSpec as P

HOPS = 4


two_pi = 2.0 * math.pi
highest = lax.Precision.HIGH
first_radix = 16


def shifted(block, axis, distance):
    devices = range(lax.axis_size(axis))
    route = [((i - distance) % len(devices), i) for i in devices]
    return lax.ppermute(block, axis, route)


def lens_step(ray_tile, fields):
    disp_x = ray_tile[..., 0, :, :]
    disp_y = ray_tile[..., 1, :, :]
    tilt_x = ray_tile[..., 2, :, :]
    tilt_y = ray_tile[..., 3, :, :]
    jac_xx = ray_tile[..., 4, :, :]
    jac_xy = ray_tile[..., 5, :, :]
    jac_yx = ray_tile[..., 6, :, :]
    jac_yy = ray_tile[..., 7, :, :]
    rate_xx = ray_tile[..., 8, :, :]
    rate_xy = ray_tile[..., 9, :, :]
    rate_yx = ray_tile[..., 10, :, :]
    rate_yy = ray_tile[..., 11, :, :]
    bend_x = fields[..., 0, :, :]
    bend_y = fields[..., 1, :, :]
    hess_xx = fields[..., 2, :, :]
    hess_yy = fields[..., 3, :, :]
    hess_xy = fields[..., 4, :, :]
    push_x = bend_x + hess_xx * disp_x + hess_xy * disp_y
    push_y = bend_y + hess_xy * disp_x + hess_yy * disp_y
    new_tilt_x = tilt_x - push_x
    new_tilt_y = tilt_y - push_y
    new_disp_x = disp_x + new_tilt_x
    new_disp_y = disp_y + new_tilt_y
    new_rate_xx = rate_xx - (hess_xx * jac_xx + hess_xy * jac_yx)
    new_rate_xy = rate_xy - (hess_xx * jac_xy + hess_xy * jac_yy)
    new_rate_yx = rate_yx - (hess_xy * jac_xx + hess_yy * jac_yx)
    new_rate_yy = rate_yy - (hess_xy * jac_xy + hess_yy * jac_yy)
    new_jac_xx = jac_xx + new_rate_xx
    new_jac_xy = jac_xy + new_rate_xy
    new_jac_yx = jac_yx + new_rate_yx
    new_jac_yy = jac_yy + new_rate_yy
    return jnp.stack(
        [
            new_disp_x,
            new_disp_y,
            new_tilt_x,
            new_tilt_y,
            new_jac_xx,
            new_jac_xy,
            new_jac_yx,
            new_jac_yy,
            new_rate_xx,
            new_rate_xy,
            new_rate_yx,
            new_rate_yy,
        ],
        axis=-3,
    )


def phase_table(left_idx, right_idx, modulus, orient):
    product = left_idx[:, None] * right_idx[None, :] % modulus
    angle = orient * two_pi / modulus * product.astype(jnp.float32)
    return (jnp.cos(angle), jnp.sin(angle))


def block_table(left_idx, right_idx, modulus, orient):
    t_re, t_im = phase_table(left_idx, right_idx, modulus, orient)
    top = jnp.concatenate([t_re, t_im], axis=1)
    bottom = jnp.concatenate([-t_im, t_re], axis=1)
    return jnp.concatenate([top, bottom], axis=0)


def mixed(form, left_op, right_op):
    return jnp.einsum(
        form, left_op, right_op, precision=highest, preferred_element_type=jnp.float32
    )


def complex_product(form, real_in, imag_in, table_re, table_im):
    if imag_in is None:
        return (mixed(form, real_in, table_re), mixed(form, real_in, table_im))
    out_re = mixed(form, real_in, table_re) - mixed(form, imag_in, table_im)
    out_im = mixed(form, real_in, table_im) + mixed(form, imag_in, table_re)
    return (out_re, out_im)


def first_factor_of(length):
    factor_one = 1
    while factor_one * factor_one < length and length % (factor_one * 2) == 0:
        factor_one = factor_one * 2
    return factor_one


def rows_forward(cells):
    row_count, length = cells.shape
    second = length // first_radix
    half = second // 2
    shaped = cells.reshape(row_count, first_radix, second)
    v_idx = jnp.arange(first_radix, dtype=jnp.int32)
    u_idx = jnp.arange(second, dtype=jnp.int32)
    m_idx = jnp.arange(half, dtype=jnp.int32)
    section_re, section_im = phase_table(v_idx, v_idx, first_radix, -1.0)
    section = jnp.concatenate([section_re, section_im], axis=1)
    part = mixed("rvu,vk->rku", shaped, section)
    part_re = part[:, :first_radix]
    part_im = part[:, first_radix:]
    twist_re, twist_im = phase_table(v_idx, u_idx, length, -1.0)
    turned_re = part_re * twist_re - part_im * twist_im
    turned_im = part_re * twist_im + part_im * twist_re
    final = block_table(u_idx, m_idx, second, -1.0)
    return mixed("rkj,jn->rkn", turned_re, final[:second]) + mixed(
        "rkj,jn->rkn", turned_im, final[second:]
    )


def columns_forward(spread_re, spread_im):
    length, col_count = spread_re.shape
    factor_one = first_factor_of(length)
    second = length // factor_one
    first_idx = jnp.arange(factor_one, dtype=jnp.int32)
    second_idx = jnp.arange(second, dtype=jnp.int32)
    section = block_table(first_idx, first_idx, factor_one, -1.0)
    part = mixed(
        "jn,jbc->nbc", section[:factor_one], spread_re.reshape(factor_one, second, col_count)
    ) + mixed(
        "jn,jbc->nbc", section[factor_one:], spread_im.reshape(factor_one, second, col_count)
    )
    part = part.reshape(2, factor_one, second, col_count)
    twist_re, twist_im = phase_table(first_idx, second_idx, length, -1.0)
    twist_re = twist_re[:, :, None]
    twist_im = twist_im[:, :, None]
    turned_re = part[0] * twist_re - part[1] * twist_im
    turned_im = part[0] * twist_im + part[1] * twist_re
    turned = jnp.stack([turned_re, turned_im], axis=1).reshape(
        factor_one, 2 * second, col_count
    )
    final = block_table(second_idx, second_idx, second, -1.0)
    done = mixed("kjc,jn->knc", turned, final)
    return done.reshape(factor_one, 2, second, col_count)


def rows_inverse(spec_re, spec_im, length, m_count):
    row_count = spec_re.shape[0]
    second = length // first_radix
    shaped_re = spec_re.reshape(row_count, first_radix, m_count)
    shaped_im = spec_im.reshape(row_count, first_radix, m_count)
    k_idx = jnp.arange(first_radix, dtype=jnp.int32)
    u_idx = jnp.arange(second, dtype=jnp.int32)
    m_idx = jnp.arange(m_count, dtype=jnp.int32)
    section_re, section_im = phase_table(m_idx, u_idx, second, 1.0)
    part_re, part_im = complex_product("rkm,mu->rku", shaped_re, shaped_im, section_re, section_im)
    twist_re, twist_im = phase_table(k_idx, u_idx, length, 1.0)
    turned_re = part_re * twist_re - part_im * twist_im
    turned_im = part_re * twist_im + part_im * twist_re
    final_re, final_im = phase_table(k_idx, k_idx, first_radix, 1.0)
    done_re, done_im = complex_product("rku,kv->rvu", turned_re, turned_im, final_re, final_im)
    return (done_re.reshape(row_count, length), done_im.reshape(row_count, length))


def wavenumbers(indices, length):
    signed = jnp.where(indices < length // 2, indices, indices - length)
    return (two_pi / length * signed.astype(jnp.float32), indices != length // 2)


def folded_spectra(spectrum, col_idx, ray_all):
    k_count, _, m_count, col_count = spectrum.shape
    length = k_count * m_count
    norm_factor = float(length * length)
    wave_col, retain_col = wavenumbers(col_idx, length)
    weight = jnp.where(col_idx == 0, 1.0, 2.0).astype(jnp.float32)
    row_idx = (
        jnp.arange(k_count, dtype=jnp.int32)[:, None]
        + k_count * jnp.arange(m_count, dtype=jnp.int32)[None, :]
    )
    wave_row, retain_row = wavenumbers(row_idx, length)
    wave_row = wave_row[:, None, :, None]
    retain_row = retain_row[:, None, :, None]
    squared = wave_col * wave_col + wave_row * wave_row
    retain = retain_row & retain_col & (squared > 0.0)
    safe_sq = jnp.where(retain, squared, 1.0)
    kernel = jnp.where(retain, -2.0 / (safe_sq * norm_factor), 0.0) * weight
    phi = kernel * spectrum
    terms = jnp.stack([phi, wave_row * phi, (wave_row * wave_row) * phi])
    terms = terms.reshape(3, k_count // ray_all, ray_all, 2, m_count, col_count)
    return jnp.transpose(jnp.sum(terms, axis=(1, 4)), (0, 2, 1, 3))


def per_device(density, lens_weight, plane_count, ray_state):
    sky_count = lax.axis_size("sky")
    sky_index = lax.axis_index("sky")
    ray_split = ray_state.shape[1] // 2
    ray_first = shifted(ray_state[:, :ray_split], "los", HOPS)
    ray_second = shifted(ray_state[:, ray_split:], "los", HOPS)
    plane_cells = density[0]
    length = plane_cells.shape[1]
    second = length // first_radix
    half = second // 2
    ray_dev = ray_state.shape[2]
    ray_all = ray_dev * sky_count
    strength = lens_weight[0] * plane_count[0].astype(jnp.float32)
    rows = rows_forward(plane_cells)
    ray_first, rows = lax.optimization_barrier((ray_first, rows))
    spread = lax.all_to_all(rows, "sky", split_axis=1, concat_axis=0, tiled=True)
    k_local = spread.shape[1]
    spread_re = spread[:, :, :half].reshape(length, k_local * half)
    spread_im = spread[:, :, half:].reshape(length, k_local * half)
    spectrum = columns_forward(spread_re, spread_im)
    ray_second, spectrum = lax.optimization_barrier((ray_second, spectrum))
    position = jnp.arange(k_local * half, dtype=jnp.int32)
    col_idx = sky_index * k_local + position // half + first_radix * (position % half)
    folds = folded_spectra(spectrum, col_idx, ray_all)
    q_idx = jnp.arange(ray_all, dtype=jnp.int32)
    back = block_table(q_idx, q_idx, ray_all, 1.0)
    at_rows = mixed("pjc,jn->pnc", folds.reshape(3, 2 * ray_all, k_local * half), back)
    at_rows = at_rows.reshape(3, 2, ray_all, k_local, half)
    returned = lax.all_to_all(at_rows, "sky", split_axis=2, concat_axis=3, tiled=True)
    k_all = returned.shape[3]
    dense = returned.reshape(3 * 2 * ray_dev, k_all * half) * strength
    arrived = jnp.stack(
        [shifted(dense, "los", HOPS - step_index) for step_index in range(HOPS)]
    ).reshape(HOPS, 3, 2, ray_dev, k_all, half)
    kx_idx = jnp.arange(k_all, dtype=jnp.int32)[:, None] + first_radix * jnp.arange(
        half, dtype=jnp.int32
    )[None, :]
    wave_col = wavenumbers(kx_idx, length)[0]
    f0_re, f0_im = arrived[:, 0, 0], arrived[:, 0, 1]
    f1_re, f1_im = arrived[:, 1, 0], arrived[:, 1, 1]
    f2_re, f2_im = arrived[:, 2, 0], arrived[:, 2, 1]
    col_sq = wave_col * wave_col
    all_re = jnp.stack(
        [-wave_col * f0_im, -f1_im, -col_sq * f0_re, -f2_re, -wave_col * f1_re], axis=1
    )
    all_im = jnp.stack(
        [wave_col * f0_re, f1_re, -col_sq * f0_im, -f2_im, -wave_col * f1_im], axis=1
    )
    flat_re = all_re.reshape(HOPS * 5 * ray_dev, k_all * half)
    flat_im = all_im.reshape(HOPS * 5 * ray_dev, k_all * half)
    field_re, _ = rows_inverse(flat_re, flat_im, length, half)
    fields = field_re.reshape(HOPS, 5, ray_dev, length)
    ray_tile = jnp.concatenate([ray_first, ray_second], axis=1)
    for step_index in range(HOPS):
        ray_tile = lens_step(ray_tile, fields[step_index][None])
    return ray_tile


def solution(mesh):
    return jax.shard_map(
        per_device,
        mesh=mesh,
        in_specs=(
            P(("real", "los"), "sky", None),
            P(("real", "los")),
            P(("real", "los")),
            P(("real", "los"), None, "sky", None),
        ),
        out_specs=P(("real", "los"), None, "sky", None),
        check_vma=False,
    )
```

profile of v0, /device:TPU:0, one launch (start us, length us, event | category | flops | bytes accessed | tf_op | source)
XLA Modules:
  0.0 219.9 jit_solution(1976992600342598660)
XLA Ops:
  0.0 2.7 %fusion.222 = (f32[1,6,16,2048]{3,2,1,0:T(8,128)}, f32[1,6,16,2048]{3,2,1,0:T(8,128)}) fusion(f32[1,12,16,2048]{3,2,1,0:T(8,128)} %param.7), kind=kLoop, calls=%fused_computation.322 | loop fusion | bytes 3145728 | tf_op jit(solution)/shard_map/slice | solution.py:205
  2.7 4.0 %collective-permute-start = (f32[1,6,16,2048]{3,2,1,0:T(8,128)}, f32[1,6,16,2048]{3,2,1,0:T(8,128)S(1)}, u32[]{:S(2)}, u32[]{:S(2)}) collective-permute-start(f32[1,6,16,2048]{3,2,1,0:T(8,128)} %get-tuple-element.84), channel_id=1, source_target_pairs={{8,0},{10,2},{12,4},{14,6},{0,8},{2,10},{4,12},{6,14},{9,1},{11,3}... | collective-permute-start | bytes 2359304 | tf_op jit(solution)/shard_map/ppermute | solution.py:19
  8.2 8.7 %copy.110 = f32[128,8,16,128]{3,2,1,0:T(8,128)} copy(f32[128,8,16,128]{3,1,2,0:T(8,128)} %bitcast.153) | data formatting | bytes 16777216
  18.2 10.2 %convolution_bitcast_fusion = f32[1024,32,128]{2,1,0:T(8,128)S(1)} fusion(f32[1024,16,128]{2,1,0:T(8,128)} %bitcast.141, f32[16,16]{1,0:T(8,128)S(1)} %get-tuple-element.91, f32[16,16]{1,0:T(8,128)S(1)} %get-tuple-element.92), kind=kOutput, calls=%fused_computation.1 | convolution fusion | flops 402653696 | bytes 25167872 | tf_op jit(solution)/shard_map/rvu,vk->rku/dot_general | solution.py:87
  28.4 7.0 %multiply_subtract_fusion = (f32[1024,16,128]{2,1,0:T(8,128)}, f32[1024,16,128]{2,1,0:T(8,128)}) fusion(f32[1024,32,128]{2,1,0:T(8,128)S(1)} %convolution_bitcast_fusion, f32[16,128]{1,0:T(8,128)S(1)} %get-tuple-element.93, f32[16,128]{1,0:T(8,128)S(1)} %get-tuple-element.94), kind=kLoop, calls=%fused_computation.10 | loop fusion | flops 12582912 | bytes 33570816 | tf_op jit(solution)/shard_map/sub | solution.py:121
  35.4 9.6 %fusion.2 = f32[1024,16,128]{2,0,1:T(8,128)S(1)} fusion(f32[1024,16,128]{2,1,0:T(8,128)} %get-tuple-element.58, f32[128,64]{1,0:T(8,128)S(1)} %get-tuple-element.96, f32[128,64]{1,0:T(8,128)S(1)} %fusion.113), kind=kOutput, calls=%fused_computation.5 | convolution fusion | flops 1610629120 | bytes 16842752 | tf_op jit(solution)/shard_map/rkj,jn->rkn/dot_general | solution.py:87
  45.1 5.6 %fusion.15 = f32[1024,16,128]{2,0,1:T(8,128)S(1)} fusion(f32[1024,16,128]{2,0,1:T(8,128)S(1)} %fusion.2, f32[1024,16,128]{2,1,0:T(8,128)S(1)} %bitcast.146, f32[128,64]{1,0:T(8,128)S(1)} %get-tuple-element.95, f32[128,64]{1,0:T(8,128)S(1)} %get-tuple-element.96), kind=kOutput, calls=%fused_computation.27 | convolution fusion | flops 1612726272 | bytes 25231360 | tf_op jit(solution)/shard_map/rkj,jn->rkn/dot_general | solution.py:87
  50.7 3.6 %fusion.9 = f32[64,32,512]{2,1,0:T(8,128)} fusion(f32[512]{0:T(512)S(1)} %get-tuple-element.104, f32[64,32]{1,0:T(8,128)S(1)} %get-tuple-element.89, f32[512]{0:T(512)S(1)} %get-tuple-element.103, pred[512]{0:T(512)(128)(4,1)S(1)} %broadcast_compare_fusion, pred[64,32]{1,0:T(8,128)(4,1)S(1)} %fusion.108), kind=kLoop, calls=%fused_computation.16 | loop fusion | flops 9437184 | bytes 4209152 | tf_op jit(solution)/shard_map/mul | solution.py:194
  54.3 4.7 %collective-permute-done = f32[1,6,16,2048]{3,2,1,0:T(8,128)S(1)} collective-permute-done((f32[1,6,16,2048]{3,2,1,0:T(8,128)}, f32[1,6,16,2048]{3,2,1,0:T(8,128)S(1)}, u32[]{:S(2)}, u32[]{:S(2)}) %collective-permute-start) | collective-permute-done | bytes 786464 | tf_op jit(solution)/shard_map/ppermute | solution.py:19
  59.0 11.0 %all_to_all.27 = f32[1024,16,128]{2,0,1:T(8,128)S(1)} all-to-all(f32[1024,16,128]{2,0,1:T(8,128)S(1)} %fusion.15), channel_id=1, replica_groups=mesh['real'=2,'los'=8,'sky'=2] {'sky'}, dimensions={1} | all-to-all | bytes 16777216 | tf_op jit(solution)/shard_map/all_to_all | solution.py:216
  70.0 4.9 %copy.84 = f32[1024,2,8,128]{3,2,0,1:T(8,128)S(1)} copy(f32[1024,2,8,128]{3,0,2,1:T(8,128)S(1)} %bitcast.148) | data formatting | bytes 16777216 | tf_op jit(solution)/shard_map/all_to_all | solution.py:216
  74.8 7.1 %fusion.220 = (f32[2048,8,64]{2,1,0:T(8,128)}, f32[2048,8,64]{2,1,0:T(8,128)}) fusion(f32[2048,8,128]{2,1,0:T(8,128)S(1)} %bitcast.140), kind=kLoop, calls=%fused_computation.320 | loop fusion | bytes 16777216 | tf_op jit(solution)/shard_map/slice | solution.py:218
  82.0 7.5 %reshape_reshape.14 = f32[64,32,512]{2,1,0:T(8,128)} reshape(f32[2048,8,64]{2,1,0:T(8,128)} %get-tuple-element.62) | data formatting | bytes 8388608 | tf_op jit(solution)/shard_map/reshape;reshape | solution.py:139
  89.5 7.5 %reshape_reshape.13 = f32[64,32,512]{2,1,0:T(8,128)} reshape(f32[2048,8,64]{2,1,0:T(8,128)} %get-tuple-element.61) | data formatting | bytes 8388608 | tf_op jit(solution)/shard_map/reshape;reshape | solution.py:137
  97.0 9.4 %fusion.10 = f32[128,32,512]{2,0,1:T(8,128)S(1)} fusion(f32[64,32,512]{2,1,0:T(8,128)} %reshape_reshape.14, f32[64,64]{1,0:T(8,128)S(1)} %get-tuple-element.97, f32[64,64]{1,0:T(8,128)S(1)} %get-tuple-element.98), kind=kOutput, calls=%fused_computation.17 | convolution fusion | flops 805314560 | bytes 12615680 | tf_op jit(solution)/shard_map/jn,jbc->nbc/dot_general | solution.py:87
  106.5 5.9 %fusion.18 = f32[128,32,512]{2,0,1:T(8,128)S(1)} fusion(f32[128,32,512]{2,0,1:T(8,128)S(1)} %fusion.10, f32[64,32,512]{2,1,0:T(8,128)S(1)} %copy-done, f32[64,64]{1,0:T(8,128)S(1)} %fusion.127, f32[64,64]{1,0:T(8,128)S(1)} %get-tuple-element.97), kind=kOutput, calls=%fused_computation.28 | convolution fusion | flops 807411712 | bytes 21004288 | tf_op jit(solution)/shard_map/jn,jbc->nbc/dot_general | solution.py:87
  115.3 8.7 %fusion = f32[64,64,512]{2,0,1:T(8,128)S(1)} fusion(f32[64,64,512]{2,0,1:T(8,128)S(1)} %bitcast.143, f32[32,32]{0,1:T(8,128)S(1)} %get-tuple-element.102, f32[32,32]{0,1:T(8,128)S(1)} %fusion.158, f32[32,32]{0,1:T(8,128)S(1)} %get-tuple-element.101), kind=kOutput, calls=%fused_computation.3 | convolution fusion | flops 805318656 | bytes 16789504 | tf_op jit(solution)/shard_map/kjc,jn->knc/dot_general | solution.py:87
  124.1 3.9 %broadcast_multiply_fusion.1 = (f32[64,2,32,512]{3,2,1,0:T(8,128)}, f32[64,2,32,512]{3,2,1,0:T(8,128)S(1)}) fusion(f32[64,32]{1,0:T(8,128)S(1)} %get-tuple-element.90, f32[64,2,32,512]{3,2,1,0:T(8,128)S(1)} %bitcast.144, f32[64,32,512]{2,1,0:T(8,128)S(1)} %copy-done.1), kind=kLoop, calls=%fused_computation.22 | loop fusion | flops 4194304 | bytes 29368320 | tf_op jit(solution)/shard_map/mul | solution.py:196
  128.6 7.4 %maximum_reduce_fusion = f32[3,32,2,512]{3,2,1,0:T(2,128)S(1)} fusion(f32[1,2,32,2,32,512]{5,4,3,2,1,0:T(8,128)S(1)} %bitcast.142, f32[1,2,32,2,32,512]{5,4,3,2,1,0:T(8,128)} %bitcast.147, f32[1,2,32,2,32,512]{5,4,3,2,1,0:T(8,128)S(1)} %bitcast.139), kind=kLoop, calls=%fused_computation | loop fusion | flops 18776064 | bytes 25559040 | tf_op jit(solution)/shard_map/reduce_sum | solution.py:198
  137.2 4.0 %all_to_all.28 = f32[2,1,49152]{2,1,0:T(1,128)S(1)} all-to-all(f32[2,1,49152]{2,1,0:T(1,128)S(1)} %reshape.941), channel_id=1, replica_groups=mesh['real'=2,'los'=8,'sky'=2] {'sky'}, dimensions={0} | all-to-all | bytes 786432 | tf_op jit(solution)/shard_map/all_to_all | solution.py:229
  144.5 4.3 %collective-permute-start.3 = (f32[96,1024]{1,0:T(8,128)S(1)}, f32[96,1024]{1,0:T(8,128)S(1)}, u32[]{:S(2)}, u32[]{:S(2)}) collective-permute-start(f32[96,1024]{1,0:T(8,128)S(1)} %mul.1429), channel_id=1, source_target_pairs={{10,0},{12,2},{14,4},{0,6},{2,8},{4,10},{6,12},{8,14},{11,1},{13,3... | collective-permute-start | bytes 1179656 | tf_op jit(solution)/shard_map/ppermute | solution.py:19
  150.8 31.0 %collective-permute-done.2 = f32[96,1024]{1,0:T(8,128)S(1)} collective-permute-done((f32[96,1024]{1,0:T(8,128)S(1)}, f32[96,1024]{1,0:T(8,128)S(1)}, u32[]{:S(2)}, u32[]{:S(2)}) %collective-permute-start.2) | collective-permute-done | bytes 393248 | tf_op jit(solution)/shard_map/ppermute | solution.py:19
  182.0 17.7 %collective-permute-done.3 = f32[96,1024]{1,0:T(8,128)S(1)} collective-permute-done((f32[96,1024]{1,0:T(8,128)S(1)}, f32[96,1024]{1,0:T(8,128)S(1)}, u32[]{:S(2)}, u32[]{:S(2)}) %collective-permute-start.3) | collective-permute-done | bytes 393248 | tf_op jit(solution)/shard_map/ppermute | solution.py:19
  212.2 2.2 add_subtract_fusion.6
  (105 shorter events, 28.8 us)
Async XLA Ops:
  2.7 56.3 %collective-permute-start = (f32[1,6,16,2048]{3,2,1,0:T(8,128)}, f32[1,6,16,2048]{3,2,1,0:T(8,128)S(1)}, u32[]{:S(2)}, u32[]{:S(2)}) collective-permute-start(f32[1,6,16,2048]{3,2,1,0:T(8,128)} %get-tuple-element.84), channel_id=1, source_target_pairs={{8,0},{10,2},{12,4},{14,6},{0,8},{2,10},{4,12},{6,14},{9,1},{11,3}... | collective-permute-start | bytes 2359304 | tf_op jit(solution)/shard_map/ppermute | solution.py:19
  6.7 117.3 %collective-permute-start.1 = (f32[1,6,16,2048]{3,2,1,0:T(8,128)}, f32[1,6,16,2048]{3,2,1,0:T(8,128)S(1)}, u32[]{:S(2)}, u32[]{:S(2)}) collective-permute-start(f32[1,6,16,2048]{3,2,1,0:T(8,128)} %get-tuple-element.85), channel_id=1, source_target_pairs={{8,0},{10,2},{12,4},{14,6},{0,8},{2,10},{4,12},{6,14},{9,1},{11,3}... | collective-permute-start | bytes 2359304 | tf_op jit(solution)/shard_map/ppermute | solution.py:19
  35.4 9.7 %slice-start = ((s8[8388608]{0:T(1024)(128)(4,1)}), s8[4194304]{0:T(1024)(128)(4,1)S(1)}, s32[]{:S(2)}) async-start(s8[8388608]{0:T(1024)(128)(4,1)} %bitcast.145), calls=%async_computation.2 | async-start | bytes 8388608
  35.4 9.7 %slice-start.1 = ((s8[8388608]{0:T(1024)(128)(4,1)}), s8[4194304]{0:T(1024)(128)(4,1)S(1)}, s32[]{:S(2)}) async-start(s8[8388608]{0:T(1024)(128)(4,1)} %bitcast.145), calls=%async_computation.3 | async-start | bytes 8388608
  59.0 11.0 %copy-start.2 = (f32[1,6,16,2048]{3,2,1,0:T(8,128)}, f32[1,6,16,2048]{3,2,1,0:T(8,128)S(1)}, u32[]{:S(2)}) copy-start(f32[1,6,16,2048]{3,2,1,0:T(8,128)S(1)} %collective-permute-done) | copy-start | bytes 2359300
  97.0 9.4 %copy-start = (f32[64,32,512]{2,1,0:T(8,128)S(1)}, f32[64,32,512]{2,1,0:T(8,128)}, u32[]{:S(2)}) copy-start(f32[64,32,512]{2,1,0:T(8,128)} %reshape_reshape.13) | copy-start | bytes 12582916
  115.3 8.8 %copy-start.1 = (f32[64,32,512]{2,1,0:T(8,128)S(1)}, f32[64,32,512]{2,1,0:T(8,128)}, u32[]{:S(2)}) copy-start(f32[64,32,512]{2,1,0:T(8,128)} %fusion.9) | copy-start | bytes 12582916
  124.1 3.9 %copy-start.3 = (f32[1,6,16,2048]{3,2,1,0:T(8,128)}, f32[1,6,16,2048]{3,2,1,0:T(8,128)S(1)}, u32[]{:S(2)}) copy-start(f32[1,6,16,2048]{3,2,1,0:T(8,128)S(1)} %collective-permute-done.1) | copy-start | bytes 2359300
  144.4 37.4 %collective-permute-start.2 = (f32[96,1024]{1,0:T(8,128)S(1)}, f32[96,1024]{1,0:T(8,128)S(1)}, u32[]{:S(2)}, u32[]{:S(2)}) collective-permute-start(f32[96,1024]{1,0:T(8,128)S(1)} %mul.1429), channel_id=1, source_target_pairs={{8,0},{10,2},{12,4},{14,6},{0,8},{2,10},{4,12},{6,14},{9,1},{11,3}... | collective-permute-start | bytes 1179656 | tf_op jit(solution)/shard_map/ppermute | solution.py:19
  144.5 55.3 %collective-permute-start.3 = (f32[96,1024]{1,0:T(8,128)S(1)}, f32[96,1024]{1,0:T(8,128)S(1)}, u32[]{:S(2)}, u32[]{:S(2)}) collective-permute-start(f32[96,1024]{1,0:T(8,128)S(1)} %mul.1429), channel_id=1, source_target_pairs={{10,0},{12,2},{14,4},{0,6},{2,8},{4,10},{6,12},{8,14},{11,1},{13,3... | collective-permute-start | bytes 1179656 | tf_op jit(solution)/shard_map/ppermute | solution.py:19
  148.8 51.2 %collective-permute-start.4 = (f32[96,1024]{1,0:T(8,128)S(1)}, f32[96,1024]{1,0:T(8,128)S(1)}, u32[]{:S(2)}, u32[]{:S(2)}) collective-permute-start(f32[96,1024]{1,0:T(8,128)S(1)} %mul.1429), channel_id=1, source_target_pairs={{12,0},{14,2},{0,4},{2,6},{4,8},{6,10},{8,12},{10,14},{13,1},{15,3... | collective-permute-start | bytes 1179656 | tf_op jit(solution)/shard_map/ppermute | solution.py:19
  149.2 50.9 %collective-permute-start.5 = (f32[96,1024]{1,0:T(8,128)S(1)}, f32[96,1024]{1,0:T(8,128)S(1)}, u32[]{:S(2)}, u32[]{:S(2)}) collective-permute-start(f32[96,1024]{1,0:T(8,128)S(1)} %mul.1429), channel_id=1, source_target_pairs={{14,0},{0,2},{2,4},{4,6},{6,8},{8,10},{10,12},{12,14},{15,1},{1,3}... | collective-permute-start | bytes 1179656 | tf_op jit(solution)/shard_map/ppermute | solution.py:19
  200.4 0.7 copy-start.10
  200.7 0.7 copy-start.9
  205.7 1.4 copy-start.8
  214.5 1.7 copy-start.4
  214.5 1.7 copy-start.5
  214.5 1.7 copy-start.6
  214.5 1.7 copy-start.7
  217.7 1.1 copy-start.11
where the time goes:
time: 224 us; the launch traced here: 220 us
  matrix products  58 us (26%)
  waiting for transfers between devices  53.5 us (24%)
  local copies, waits for them, and re-layouts  44.3 us (20%)
  other arithmetic  37.6 us (17%)
  blocking collectives  15 us (7%)
  starting transfers between devices  9.21 us (4%)
  between operations  2.35 us (1%)
    dot_general x13, matrix products, mixed(): jnp.einsum(form, left_op, right_op, precision=highest, preferred_element_...  58 us
    ppermute x6, waiting for transfers between devices, shifted(): return lax.ppermute(block, axis, route)  53.5 us
    unnamed x36, local copies, waits for them, and re-layouts  11.4 us
    all_to_all x1, blocking collectives, per_device(): lax.all_to_all(rows, 'sky', split_axis=1, concat_axis=0, tiled=True)  11 us
    ppermute x6, starting transfers between devices, shifted(): return lax.ppermute(block, axis, route)  9.21 us
    another operation x1, local copies, waits for them, and re-layouts, columns_forward(): spread_re.reshape(factor_one, second, col_count)  7.52 us
    another operation x1, local copies, waits for them, and re-layouts, columns_forward(): spread_im.reshape(factor_one, second, col_count)  7.51 us
    reduce_sum x1, other arithmetic, folded_spectra(): return jnp.transpose(jnp.sum(terms, axis=(1, 4)), (0, 2, 1, 3))  7.37 us
  transfers between devices with their start and end apart: 6, of which 3 were waited for; matrix products, arithmetic and copies ran while one was open for 46% of the time, Pallas kernels for 0%

commit v1 on v0

--- a/solution.py
+++ b/solution.py
@@ -144,11 +144,10 @@
     twist_im = twist_im[:, :, None]
     turned_re = part[0] * twist_re - part[1] * twist_im
     turned_im = part[0] * twist_im + part[1] * twist_re
-    turned = jnp.stack([turned_re, turned_im], axis=1).reshape(
-        factor_one, 2 * second, col_count
-    )
     final = block_table(second_idx, second_idx, second, -1.0)
-    done = mixed("kjc,jn->knc", turned, final)
+    done = mixed("kjc,jn->knc", turned_re, final[:second]) + mixed(
+        "kjc,jn->knc", turned_im, final[second:]
+    )
     return done.reshape(factor_one, 2, second, col_count)
 
 

time: 224 us -> 226 us (level)
  matrix products: 58 us -> 61.5 us
    dot_general x13 -> x14, matrix products: 58 us -> 61.5 us  [mixed(): jnp.einsum(form, left_op, right_op, precision=highest, preferred_element_...]
    another operation x2 -> x0, other arithmetic: 2.92 us -> none  [columns_forward(): jnp.stack([turned_re, turned_im], axis=1)]
  transfers between devices with their start and end apart: 6 -> 6, of which waited for: 3 -> 3; matrix products, arithmetic and copies ran while one was open for 46% -> 47% of each run, Pallas kernels for 0% -> 0%
where the time goes in v1:
time: 226 us; the launch traced here: 222 us
  matrix products  61.5 us (27%)
  waiting for transfers between devices  53.7 us (24%)
  local copies, waits for them, and re-layouts  44.3 us (20%)
  other arithmetic  36 us (16%)
  blocking collectives  15 us (7%)
  starting transfers between devices  9.02 us (4%)
  between operations  2.36 us (1%)
    dot_general x14, matrix products, mixed(): jnp.einsum(form, left_op, right_op, precision=highest, preferred_element_...  61.5 us
    ppermute x6, waiting for transfers between devices, shifted(): return lax.ppermute(block, axis, route)  53.7 us
    unnamed x36, local copies, waits for them, and re-layouts  11.4 us
    all_to_all x1, blocking collectives, per_device(): lax.all_to_all(rows, 'sky', split_axis=1, concat_axis=0, tiled=True)  10.9 us
    ppermute x6, starting transfers between devices, shifted(): return lax.ppermute(block, axis, route)  9.02 us
    another operation x1, local copies, waits for them, and re-layouts, columns_forward(): spread_re.reshape(factor_one, second, col_count)  7.52 us
    another operation x1, local copies, waits for them, and re-layouts, columns_forward(): spread_im.reshape(factor_one, second, col_count)  7.51 us
    reduce_sum x1, other arithmetic, folded_spectra(): return jnp.transpose(jnp.sum(terms, axis=(1, 4)), (0, 2, 1, 3))  7.37 us
  transfers between devices with their start and end apart: 6, of which 3 were waited for; matrix products, arithmetic and copies ran while one was open for 47% of the time, Pallas kernels for 0%

profile of v1, /device:TPU:0, one launch (start us, length us, event | category | flops | bytes accessed | tf_op | source)
XLA Modules:
  0.0 221.8 jit_solution(15657161306616747982)
XLA Ops:
  0.0 2.7 %fusion.226 = (f32[1,6,16,2048]{3,2,1,0:T(8,128)}, f32[1,6,16,2048]{3,2,1,0:T(8,128)}) fusion(f32[1,12,16,2048]{3,2,1,0:T(8,128)} %param.7), kind=kLoop, calls=%fused_computation.324 | loop fusion | bytes 3145728 | tf_op jit(solution)/shard_map/slice | solution.py:204
  2.7 4.0 %collective-permute-start = (f32[1,6,16,2048]{3,2,1,0:T(8,128)}, f32[1,6,16,2048]{3,2,1,0:T(8,128)S(1)}, u32[]{:S(2)}, u32[]{:S(2)}) collective-permute-start(f32[1,6,16,2048]{3,2,1,0:T(8,128)} %get-tuple-element.84), channel_id=1, source_target_pairs={{8,0},{10,2},{12,4},{14,6},{0,8},{2,10},{4,12},{6,14},{9,1},{11,3}... | collective-permute-start | bytes 2359304 | tf_op jit(solution)/shard_map/ppermute | solution.py:19
  8.2 8.7 %copy.122 = f32[128,8,16,128]{3,2,1,0:T(8,128)} copy(f32[128,8,16,128]{3,1,2,0:T(8,128)} %bitcast.150) | data formatting | bytes 16777216
  18.2 10.2 %convolution_bitcast_fusion = f32[1024,32,128]{2,1,0:T(8,128)S(1)} fusion(f32[1024,16,128]{2,1,0:T(8,128)} %bitcast.139, f32[16,16]{1,0:T(8,128)S(1)} %get-tuple-element.91, f32[16,16]{1,0:T(8,128)S(1)} %get-tuple-element.92), kind=kOutput, calls=%fused_computation.1 | convolution fusion | flops 402653696 | bytes 25167872 | tf_op jit(solution)/shard_map/rvu,vk->rku/dot_general | solution.py:87
  28.4 7.0 %multiply_subtract_fusion = (f32[1024,16,128]{2,1,0:T(8,128)}, f32[1024,16,128]{2,1,0:T(8,128)}) fusion(f32[1024,32,128]{2,1,0:T(8,128)S(1)} %convolution_bitcast_fusion, f32[16,128]{1,0:T(8,128)S(1)} %get-tuple-element.93, f32[16,128]{1,0:T(8,128)S(1)} %get-tuple-element.94), kind=kLoop, calls=%fused_computation.7 | loop fusion | flops 12582912 | bytes 33570816 | tf_op jit(solution)/shard_map/sub | solution.py:121
  35.4 9.6 %fusion = f32[1024,16,128]{2,0,1:T(8,128)S(1)} fusion(f32[1024,16,128]{2,1,0:T(8,128)} %get-tuple-element.58, f32[128,64]{1,0:T(8,128)S(1)} %get-tuple-element.96, f32[128,64]{1,0:T(8,128)S(1)} %fusion.112), kind=kOutput, calls=%fused_computation.2 | convolution fusion | flops 1610629120 | bytes 16842752 | tf_op jit(solution)/shard_map/rkj,jn->rkn/dot_general | solution.py:87
  45.1 5.6 %fusion.17 = f32[1024,16,128]{2,0,1:T(8,128)S(1)} fusion(f32[1024,16,128]{2,0,1:T(8,128)S(1)} %fusion, f32[1024,16,128]{2,1,0:T(8,128)S(1)} %bitcast.143, f32[128,64]{1,0:T(8,128)S(1)} %get-tuple-element.95, f32[128,64]{1,0:T(8,128)S(1)} %get-tuple-element.96), kind=kOutput, calls=%fused_computation.28 | convolution fusion | flops 1612726272 | bytes 25231360 | tf_op jit(solution)/shard_map/rkj,jn->rkn/dot_general | solution.py:87
  50.7 3.6 %fusion.7 = f32[64,32,512]{2,1,0:T(8,128)} fusion(f32[512]{0:T(512)S(1)} %get-tuple-element.104, f32[64,32]{1,0:T(8,128)S(1)} %get-tuple-element.89, f32[512]{0:T(512)S(1)} %get-tuple-element.103, pred[512]{0:T(512)(128)(4,1)S(1)} %broadcast_compare_fusion, pred[64,32]{1,0:T(8,128)(4,1)S(1)} %fusion.107), kind=kLoop, calls=%fused_computation.13 | loop fusion | flops 9437184 | bytes 4209152 | tf_op jit(solution)/shard_map/mul | solution.py:193
  54.3 4.7 %collective-permute-done = f32[1,6,16,2048]{3,2,1,0:T(8,128)S(1)} collective-permute-done((f32[1,6,16,2048]{3,2,1,0:T(8,128)}, f32[1,6,16,2048]{3,2,1,0:T(8,128)S(1)}, u32[]{:S(2)}, u32[]{:S(2)}) %collective-permute-start) | collective-permute-done | bytes 786464 | tf_op jit(solution)/shard_map/ppermute | solution.py:19
  59.0 10.9 %all_to_all.27 = f32[1024,16,128]{2,0,1:T(8,128)S(1)} all-to-all(f32[1024,16,128]{2,0,1:T(8,128)S(1)} %fusion.17), channel_id=1, replica_groups=mesh['real'=2,'los'=8,'sky'=2] {'sky'}, dimensions={1} | all-to-all | bytes 16777216 | tf_op jit(solution)/shard_map/all_to_all | solution.py:215
  69.9 4.9 %copy.92 = f32[1024,2,8,128]{3,2,0,1:T(8,128)S(1)} copy(f32[1024,2,8,128]{3,0,2,1:T(8,128)S(1)} %bitcast.145) | data formatting | bytes 16777216 | tf_op jit(solution)/shard_map/all_to_all | solution.py:215
  74.8 7.1 %fusion.224 = (f32[2048,8,64]{2,1,0:T(8,128)}, f32[2048,8,64]{2,1,0:T(8,128)}) fusion(f32[2048,8,128]{2,1,0:T(8,128)S(1)} %bitcast.138), kind=kLoop, calls=%fused_computation.322 | loop fusion | bytes 16777216 | tf_op jit(solution)/shard_map/slice | solution.py:217
  81.9 7.5 %reshape_reshape.14 = f32[64,32,512]{2,1,0:T(8,128)} reshape(f32[2048,8,64]{2,1,0:T(8,128)} %get-tuple-element.62) | data formatting | bytes 8388608 | tf_op jit(solution)/shard_map/reshape;reshape | solution.py:139
  89.4 7.5 %reshape_reshape.13 = f32[64,32,512]{2,1,0:T(8,128)} reshape(f32[2048,8,64]{2,1,0:T(8,128)} %get-tuple-element.61) | data formatting | bytes 8388608 | tf_op jit(solution)/shard_map/reshape;reshape | solution.py:137
  96.9 9.4 %fusion.12 = f32[128,32,512]{2,0,1:T(8,128)S(1)} fusion(f32[64,32,512]{2,1,0:T(8,128)} %reshape_reshape.14, f32[64,64]{1,0:T(8,128)S(1)} %get-tuple-element.97, f32[64,64]{1,0:T(8,128)S(1)} %get-tuple-element.98), kind=kOutput, calls=%fused_computation.18 | convolution fusion | flops 805314560 | bytes 12615680 | tf_op jit(solution)/shard_map/jn,jbc->nbc/dot_general | solution.py:87
  106.4 5.9 %fusion.20 = f32[128,32,512]{2,0,1:T(8,128)S(1)} fusion(f32[128,32,512]{2,0,1:T(8,128)S(1)} %fusion.12, f32[64,32,512]{2,1,0:T(8,128)S(1)} %copy-done, f32[64,64]{1,0:T(8,128)S(1)} %fusion.130, f32[64,64]{1,0:T(8,128)S(1)} %get-tuple-element.97), kind=kOutput, calls=%fused_computation.29 | convolution fusion | flops 807411712 | bytes 21004288 | tf_op jit(solution)/shard_map/jn,jbc->nbc/dot_general | solution.py:87
  113.4 6.0 %fusion.8 = f32[64,64,512]{2,0,1:T(8,128)S(1)} fusion(f32[64,32,512]{2,0,1:T(8,128)S(1)} %get-tuple-element.60, f32[32,32]{1,0:T(8,128)S(1)} %get-tuple-element.101, f32[32,32]{1,0:T(8,128)S(1)} %get-tuple-element.102), kind=kOutput, calls=%fused_computation.14 | convolution fusion | flops 402655232 | bytes 12591104 | tf_op jit(solution)/shard_map/kjc,jn->knc/dot_general | solution.py:87
  119.4 6.2 %fusion.23 = f32[64,64,512]{2,0,1:T(8,128)S(1)} fusion(f32[64,64,512]{2,0,1:T(8,128)S(1)} %fusion.8, f32[64,32,512]{2,0,1:T(8,128)S(1)} %get-tuple-element.59, f32[32,32]{1,0:T(8,128)S(1)} %multiply_sine_fusion, f32[32,32]{1,0:T(8,128)S(1)} %get-tuple-element.101), kind=kOutput, calls=%fused_computation.30 | convolution fusion | flops 404752384 | bytes 20979712 | tf_op jit(solution)/shard_map/kjc,jn->knc/dot_general | solution.py:87
  125.7 4.1 %broadcast_multiply_fusion.1 = (f32[64,2,32,512]{3,2,1,0:T(8,128)}, f32[64,2,32,512]{3,2,1,0:T(8,128)S(1)}) fusion(f32[64,32]{1,0:T(8,128)S(1)} %get-tuple-element.90, f32[64,2,32,512]{3,2,1,0:T(8,128)S(1)} %bitcast.141, f32[64,32,512]{2,1,0:T(8,128)S(1)} %copy-done.1), kind=kLoop, calls=%fused_computation.23 | loop fusion | flops 4194304 | bytes 29368320 | tf_op jit(solution)/shard_map/mul | solution.py:195
  130.4 7.4 %maximum_reduce_fusion = f32[3,32,2,512]{3,2,1,0:T(2,128)S(1)} fusion(f32[1,2,32,2,32,512]{5,4,3,2,1,0:T(8,128)S(1)} %bitcast.140, f32[1,2,32,2,32,512]{5,4,3,2,1,0:T(8,128)} %bitcast.144, f32[1,2,32,2,32,512]{5,4,3,2,1,0:T(8,128)S(1)} %bitcast.137), kind=kLoop, calls=%fused_computation | loop fusion | flops 18776064 | bytes 25559040 | tf_op jit(solution)/shard_map/reduce_sum | solution.py:197
  139.1 4.0 %all_to_all.28 = f32[2,1,49152]{2,1,0:T(1,128)S(1)} all-to-all(f32[2,1,49152]{2,1,0:T(1,128)S(1)} %reshape.938), channel_id=1, replica_groups=mesh['real'=2,'los'=8,'sky'=2] {'sky'}, dimensions={0} | all-to-all | bytes 786432 | tf_op jit(solution)/shard_map/all_to_all | solution.py:228
  146.3 4.3 %collective-permute-start.3 = (f32[96,1024]{1,0:T(8,128)S(1)}, f32[96,1024]{1,0:T(8,128)S(1)}, u32[]{:S(2)}, u32[]{:S(2)}) collective-permute-start(f32[96,1024]{1,0:T(8,128)S(1)} %mul.1429), channel_id=1, source_target_pairs={{10,0},{12,2},{14,4},{0,6},{2,8},{4,10},{6,12},{8,14},{11,1},{13,3... | collective-permute-start | bytes 1179656 | tf_op jit(solution)/shard_map/ppermute | solution.py:19
  152.5 31.2 %collective-permute-done.2 = f32[96,1024]{1,0:T(8,128)S(1)} collective-permute-done((f32[96,1024]{1,0:T(8,128)S(1)}, f32[96,1024]{1,0:T(8,128)S(1)}, u32[]{:S(2)}, u32[]{:S(2)}) %collective-permute-start.2) | collective-permute-done | bytes 393248 | tf_op jit(solution)/shard_map/ppermute | solution.py:19
  183.9 17.7 %collective-permute-done.3 = f32[96,1024]{1,0:T(8,128)S(1)} collective-permute-done((f32[96,1024]{1,0:T(8,128)S(1)}, f32[96,1024]{1,0:T(8,128)S(1)}, u32[]{:S(2)}, u32[]{:S(2)}) %collective-permute-start.3) | collective-permute-done | bytes 393248 | tf_op jit(solution)/shard_map/ppermute | solution.py:19
  (105 shorter events, 29.1 us)
Async XLA Ops:
  2.7 56.3 %collective-permute-start = (f32[1,6,16,2048]{3,2,1,0:T(8,128)}, f32[1,6,16,2048]{3,2,1,0:T(8,128)S(1)}, u32[]{:S(2)}, u32[]{:S(2)}) collective-permute-start(f32[1,6,16,2048]{3,2,1,0:T(8,128)} %get-tuple-element.84), channel_id=1, source_target_pairs={{8,0},{10,2},{12,4},{14,6},{0,8},{2,10},{4,12},{6,14},{9,1},{11,3}... | collective-permute-start | bytes 2359304 | tf_op jit(solution)/shard_map/ppermute | solution.py:19
  6.7 118.9 %collective-permute-start.1 = (f32[1,6,16,2048]{3,2,1,0:T(8,128)}, f32[1,6,16,2048]{3,2,1,0:T(8,128)S(1)}, u32[]{:S(2)}, u32[]{:S(2)}) collective-permute-start(f32[1,6,16,2048]{3,2,1,0:T(8,128)} %get-tuple-element.85), channel_id=1, source_target_pairs={{8,0},{10,2},{12,4},{14,6},{0,8},{2,10},{4,12},{6,14},{9,1},{11,3}... | collective-permute-start | bytes 2359304 | tf_op jit(solution)/shard_map/ppermute | solution.py:19
  35.4 9.6 %slice-start = ((s8[8388608]{0:T(1024)(128)(4,1)}), s8[4194304]{0:T(1024)(128)(4,1)S(1)}, s32[]{:S(2)}) async-start(s8[8388608]{0:T(1024)(128)(4,1)} %bitcast.142), calls=%async_computation.2 | async-start | bytes 8388608
  35.4 9.7 %slice-start.1 = ((s8[8388608]{0:T(1024)(128)(4,1)}), s8[4194304]{0:T(1024)(128)(4,1)S(1)}, s32[]{:S(2)}) async-start(s8[8388608]{0:T(1024)(128)(4,1)} %bitcast.142), calls=%async_computation.3 | async-start | bytes 8388608
  59.0 10.9 %copy-start.2 = (f32[1,6,16,2048]{3,2,1,0:T(8,128)}, f32[1,6,16,2048]{3,2,1,0:T(8,128)S(1)}, u32[]{:S(2)}) copy-start(f32[1,6,16,2048]{3,2,1,0:T(8,128)S(1)} %collective-permute-done) | copy-start | bytes 2359300
  96.9 9.4 %copy-start = (f32[64,32,512]{2,1,0:T(8,128)S(1)}, f32[64,32,512]{2,1,0:T(8,128)}, u32[]{:S(2)}) copy-start(f32[64,32,512]{2,1,0:T(8,128)} %reshape_reshape.13) | copy-start | bytes 12582916
  119.4 6.2 %copy-start.1 = (f32[64,32,512]{2,1,0:T(8,128)S(1)}, f32[64,32,512]{2,1,0:T(8,128)}, u32[]{:S(2)}) copy-start(f32[64,32,512]{2,1,0:T(8,128)} %fusion.7) | copy-start | bytes 12582916
  125.6 4.1 %copy-start.3 = (f32[1,6,16,2048]{3,2,1,0:T(8,128)}, f32[1,6,16,2048]{3,2,1,0:T(8,128)S(1)}, u32[]{:S(2)}) copy-start(f32[1,6,16,2048]{3,2,1,0:T(8,128)S(1)} %collective-permute-done.1) | copy-start | bytes 2359300
  146.2 37.4 %collective-permute-start.2 = (f32[96,1024]{1,0:T(8,128)S(1)}, f32[96,1024]{1,0:T(8,128)S(1)}, u32[]{:S(2)}, u32[]{:S(2)}) collective-permute-start(f32[96,1024]{1,0:T(8,128)S(1)} %mul.1429), channel_id=1, source_target_pairs={{8,0},{10,2},{12,4},{14,6},{0,8},{2,10},{4,12},{6,14},{9,1},{11,3}... | collective-permute-start | bytes 1179656 | tf_op jit(solution)/shard_map/ppermute | solution.py:19
  146.3 55.3 %collective-permute-start.3 = (f32[96,1024]{1,0:T(8,128)S(1)}, f32[96,1024]{1,0:T(8,128)S(1)}, u32[]{:S(2)}, u32[]{:S(2)}) collective-permute-start(f32[96,1024]{1,0:T(8,128)S(1)} %mul.1429), channel_id=1, source_target_pairs={{10,0},{12,2},{14,4},{0,6},{2,8},{4,10},{6,12},{8,14},{11,1},{13,3... | collective-permute-start | bytes 1179656 | tf_op jit(solution)/shard_map/ppermute | solution.py:19
  150.6 51.2 %collective-permute-start.4 = (f32[96,1024]{1,0:T(8,128)S(1)}, f32[96,1024]{1,0:T(8,128)S(1)}, u32[]{:S(2)}, u32[]{:S(2)}) collective-permute-start(f32[96,1024]{1,0:T(8,128)S(1)} %mul.1429), channel_id=1, source_target_pairs={{12,0},{14,2},{0,4},{2,6},{4,8},{6,10},{8,12},{10,14},{13,1},{15,3... | collective-permute-start | bytes 1179656 | tf_op jit(solution)/shard_map/ppermute | solution.py:19
  151.1 51.0 %collective-permute-start.5 = (f32[96,1024]{1,0:T(8,128)S(1)}, f32[96,1024]{1,0:T(8,128)S(1)}, u32[]{:S(2)}, u32[]{:S(2)}) collective-permute-start(f32[96,1024]{1,0:T(8,128)S(1)} %mul.1429), channel_id=1, source_target_pairs={{14,0},{0,2},{2,4},{4,6},{6,8},{8,10},{10,12},{12,14},{15,1},{1,3}... | collective-permute-start | bytes 1179656 | tf_op jit(solution)/shard_map/ppermute | solution.py:19
  202.3 0.7 copy-start.10
  202.6 0.7 copy-start.9
  207.5 1.4 copy-start.8
  216.4 1.7 copy-start.4
  216.4 1.7 copy-start.5
  216.4 1.7 copy-start.6
  216.4 1.7 copy-start.7
  219.6 1.1 copy-start.11

commit v2 on v0

--- a/solution.py
+++ b/solution.py
@@ -201,7 +201,7 @@
 def per_device(density, lens_weight, plane_count, ray_state):
     sky_count = lax.axis_size("sky")
     sky_index = lax.axis_index("sky")
-    ray_split = ray_state.shape[1] // 2
+    ray_split = ray_state.shape[1] // 3
     ray_first = shifted(ray_state[:, :ray_split], "los", HOPS)
     ray_second = shifted(ray_state[:, ray_split:], "los", HOPS)
     plane_cells = density[0]

time: 224 us -> 220 us (0.982)
  waiting for transfers between devices: 53.5 us -> 47.5 us
    ppermute x6, waiting for transfers between devices: 53.5 us -> 47.5 us  [shifted(): return lax.ppermute(block, axis, route)]
    slice x0 -> x1, local copies, waits for them, and re-layouts: none -> 2.29 us  [per_device(): ray_second = shifted(ray_state[:, ray_split:], 'los', HOPS)]
    unnamed x36 -> x38, local copies, waits for them, and re-layouts: 11.4 us -> 11.4 us
  transfers between devices with their start and end apart: 6 -> 6, of which waited for: 3 -> 2; matrix products, arithmetic and copies ran while one was open for 46% -> 48% of each run, Pallas kernels for 0% -> 0%
where the time goes in v2:
time: 220 us; the launch traced here: 216 us
  matrix products  58 us (26%)
  waiting for transfers between devices  47.5 us (22%)
  local copies, waits for them, and re-layouts  45.8 us (21%)
  other arithmetic  36.5 us (17%)
  blocking collectives  15 us (7%)
  starting transfers between devices  10.6 us (5%)
  between operations  2.36 us (1%)
    dot_general x13, matrix products, mixed(): jnp.einsum(form, left_op, right_op, precision=highest, preferred_element_...  58 us
    ppermute x6, waiting for transfers between devices, shifted(): return lax.ppermute(block, axis, route)  47.5 us
    unnamed x38, local copies, waits for them, and re-layouts  11.4 us
    all_to_all x1, blocking collectives, per_device(): lax.all_to_all(rows, 'sky', split_axis=1, concat_axis=0, tiled=True)  11 us
    ppermute x6, starting transfers between devices, shifted(): return lax.ppermute(block, axis, route)  10.6 us
    another operation x1, local copies, waits for them, and re-layouts, columns_forward(): spread_re.reshape(factor_one, second, col_count)  7.52 us
    another operation x1, local copies, waits for them, and re-layouts, columns_forward(): spread_im.reshape(factor_one, second, col_count)  7.51 us
    reduce_sum x1, other arithmetic, folded_spectra(): return jnp.transpose(jnp.sum(terms, axis=(1, 4)), (0, 2, 1, 3))  7.37 us
  transfers between devices with their start and end apart: 6, of which 2 were waited for; matrix products, arithmetic and copies ran while one was open for 48% of the time, Pallas kernels for 0%

profile of v2, /device:TPU:0, one launch (start us, length us, event | category | flops | bytes accessed | tf_op | source)
XLA Modules:
  0.0 215.7 jit_solution(1923841776148195720)
XLA Ops:
  1.9 4.0 %collective-permute-start = (f32[1,4,16,2048]{3,2,1,0:T(8,128)}, f32[1,4,16,2048]{3,2,1,0:T(8,128)S(1)}, u32[]{:S(2)}, u32[]{:S(2)}) collective-permute-start(f32[1,4,16,2048]{3,2,1,0:T(8,128)} %slice.166), channel_id=1, source_target_pairs={{8,0},{10,2},{12,4},{14,6},{0,8},{2,10},{4,12},{6,14},{9,1},{11,3}... | collective-permute-start | bytes 1572872 | tf_op jit(solution)/shard_map/ppermute | solution.py:19
  5.9 2.3 %slice.171 = f32[1,8,16,2048]{3,2,1,0:T(8,128)} slice(f32[1,12,16,2048]{3,2,1,0:T(8,128)} %param.7), slice={[0:1], [4:12], [0:16], [0:2048]} | slice | bytes 2097152 | tf_op jit(solution)/shard_map/slice | solution.py:206
  9.7 8.7 %copy.110 = f32[128,8,16,128]{3,2,1,0:T(8,128)} copy(f32[128,8,16,128]{3,1,2,0:T(8,128)} %bitcast.153) | data formatting | bytes 16777216
  19.7 10.2 %convolution_bitcast_fusion = f32[1024,32,128]{2,1,0:T(8,128)S(1)} fusion(f32[1024,16,128]{2,1,0:T(8,128)} %bitcast.141, f32[16,16]{1,0:T(8,128)S(1)} %get-tuple-element.89, f32[16,16]{1,0:T(8,128)S(1)} %get-tuple-element.90), kind=kOutput, calls=%fused_computation.1 | convolution fusion | flops 402653696 | bytes 25167872 | tf_op jit(solution)/shard_map/rvu,vk->rku/dot_general | solution.py:87
  29.9 7.0 %multiply_subtract_fusion = (f32[1024,16,128]{2,1,0:T(8,128)}, f32[1024,16,128]{2,1,0:T(8,128)}) fusion(f32[1024,32,128]{2,1,0:T(8,128)S(1)} %convolution_bitcast_fusion, f32[16,128]{1,0:T(8,128)S(1)} %get-tuple-element.91, f32[16,128]{1,0:T(8,128)S(1)} %get-tuple-element.92), kind=kLoop, calls=%fused_computation.10 | loop fusion | flops 12582912 | bytes 33570816 | tf_op jit(solution)/shard_map/sub | solution.py:121
  36.9 9.6 %fusion.2 = f32[1024,16,128]{2,0,1:T(8,128)S(1)} fusion(f32[1024,16,128]{2,1,0:T(8,128)} %get-tuple-element.58, f32[128,64]{1,0:T(8,128)S(1)} %get-tuple-element.94, f32[128,64]{1,0:T(8,128)S(1)} %fusion.113), kind=kOutput, calls=%fused_computation.5 | convolution fusion | flops 1610629120 | bytes 16842752 | tf_op jit(solution)/shard_map/rkj,jn->rkn/dot_general | solution.py:87
  46.6 5.6 %fusion.15 = f32[1024,16,128]{2,0,1:T(8,128)S(1)} fusion(f32[1024,16,128]{2,0,1:T(8,128)S(1)} %fusion.2, f32[1024,16,128]{2,1,0:T(8,128)S(1)} %bitcast.146, f32[128,64]{1,0:T(8,128)S(1)} %get-tuple-element.93, f32[128,64]{1,0:T(8,128)S(1)} %get-tuple-element.94), kind=kOutput, calls=%fused_computation.27 | convolution fusion | flops 1612726272 | bytes 25231360 | tf_op jit(solution)/shard_map/rkj,jn->rkn/dot_general | solution.py:87
  52.2 3.6 %fusion.9 = f32[64,32,512]{2,1,0:T(8,128)} fusion(f32[512]{0:T(512)S(1)} %get-tuple-element.102, f32[64,32]{1,0:T(8,128)S(1)} %get-tuple-element.87, f32[512]{0:T(512)S(1)} %get-tuple-element.101, pred[512]{0:T(512)(128)(4,1)S(1)} %broadcast_compare_fusion, pred[64,32]{1,0:T(8,128)(4,1)S(1)} %fusion.108), kind=kLoop, calls=%fused_computation.16 | loop fusion | flops 9437184 | bytes 4209152 | tf_op jit(solution)/shard_map/mul | solution.py:194
  55.7 11.0 %all_to_all.27 = f32[1024,16,128]{2,0,1:T(8,128)S(1)} all-to-all(f32[1024,16,128]{2,0,1:T(8,128)S(1)} %fusion.15), channel_id=1, replica_groups=mesh['real'=2,'los'=8,'sky'=2] {'sky'}, dimensions={1} | all-to-all | bytes 16777216 | tf_op jit(solution)/shard_map/all_to_all | solution.py:216
  66.7 4.9 %copy.84 = f32[1024,2,8,128]{3,2,0,1:T(8,128)S(1)} copy(f32[1024,2,8,128]{3,0,2,1:T(8,128)S(1)} %bitcast.148) | data formatting | bytes 16777216 | tf_op jit(solution)/shard_map/all_to_all | solution.py:216
  71.6 7.1 %fusion.220 = (f32[2048,8,64]{2,1,0:T(8,128)}, f32[2048,8,64]{2,1,0:T(8,128)}) fusion(f32[2048,8,128]{2,1,0:T(8,128)S(1)} %bitcast.140), kind=kLoop, calls=%fused_computation.320 | loop fusion | bytes 16777216 | tf_op jit(solution)/shard_map/slice | solution.py:218
  78.7 7.5 %reshape_reshape.14 = f32[64,32,512]{2,1,0:T(8,128)} reshape(f32[2048,8,64]{2,1,0:T(8,128)} %get-tuple-element.62) | data formatting | bytes 8388608 | tf_op jit(solution)/shard_map/reshape;reshape | solution.py:139
  86.2 7.5 %reshape_reshape.13 = f32[64,32,512]{2,1,0:T(8,128)} reshape(f32[2048,8,64]{2,1,0:T(8,128)} %get-tuple-element.61) | data formatting | bytes 8388608 | tf_op jit(solution)/shard_map/reshape;reshape | solution.py:137
  93.8 9.4 %fusion.10 = f32[128,32,512]{2,0,1:T(8,128)S(1)} fusion(f32[64,32,512]{2,1,0:T(8,128)} %reshape_reshape.14, f32[64,64]{1,0:T(8,128)S(1)} %get-tuple-element.95, f32[64,64]{1,0:T(8,128)S(1)} %get-tuple-element.96), kind=kOutput, calls=%fused_computation.17 | convolution fusion | flops 805314560 | bytes 12615680 | tf_op jit(solution)/shard_map/jn,jbc->nbc/dot_general | solution.py:87
  103.2 5.9 %fusion.18 = f32[128,32,512]{2,0,1:T(8,128)S(1)} fusion(f32[128,32,512]{2,0,1:T(8,128)S(1)} %fusion.10, f32[64,32,512]{2,1,0:T(8,128)S(1)} %copy-done, f32[64,64]{1,0:T(8,128)S(1)} %fusion.127, f32[64,64]{1,0:T(8,128)S(1)} %get-tuple-element.95), kind=kOutput, calls=%fused_computation.28 | convolution fusion | flops 807411712 | bytes 21004288 | tf_op jit(solution)/shard_map/jn,jbc->nbc/dot_general | solution.py:87
  112.1 8.7 %fusion = f32[64,64,512]{2,0,1:T(8,128)S(1)} fusion(f32[64,64,512]{2,0,1:T(8,128)S(1)} %bitcast.143, f32[32,32]{0,1:T(8,128)S(1)} %get-tuple-element.100, f32[32,32]{0,1:T(8,128)S(1)} %fusion.158, f32[32,32]{0,1:T(8,128)S(1)} %get-tuple-element.99), kind=kOutput, calls=%fused_computation.3 | convolution fusion | flops 805318656 | bytes 16789504 | tf_op jit(solution)/shard_map/kjc,jn->knc/dot_general | solution.py:87
  120.8 4.0 %broadcast_multiply_fusion.1 = (f32[64,2,32,512]{3,2,1,0:T(8,128)}, f32[64,2,32,512]{3,2,1,0:T(8,128)S(1)}) fusion(f32[64,32]{1,0:T(8,128)S(1)} %get-tuple-element.88, f32[64,2,32,512]{3,2,1,0:T(8,128)S(1)} %bitcast.144, f32[64,32,512]{2,1,0:T(8,128)S(1)} %copy-done.1), kind=kLoop, calls=%fused_computation.22 | loop fusion | flops 4194304 | bytes 29368320 | tf_op jit(solution)/shard_map/mul | solution.py:196
  125.5 7.4 %maximum_reduce_fusion = f32[3,32,2,512]{3,2,1,0:T(2,128)S(1)} fusion(f32[1,2,32,2,32,512]{5,4,3,2,1,0:T(8,128)S(1)} %bitcast.142, f32[1,2,32,2,32,512]{5,4,3,2,1,0:T(8,128)} %bitcast.147, f32[1,2,32,2,32,512]{5,4,3,2,1,0:T(8,128)S(1)} %bitcast.139), kind=kLoop, calls=%fused_computation | loop fusion | flops 18776064 | bytes 25559040 | tf_op jit(solution)/shard_map/reduce_sum | solution.py:198
  134.0 4.0 %all_to_all.28 = f32[2,1,49152]{2,1,0:T(1,128)S(1)} all-to-all(f32[2,1,49152]{2,1,0:T(1,128)S(1)} %reshape.941), channel_id=1, replica_groups=mesh['real'=2,'los'=8,'sky'=2] {'sky'}, dimensions={0} | all-to-all | bytes 786432 | tf_op jit(solution)/shard_map/all_to_all | solution.py:229
  141.2 3.0 %collective-permute-start.2 = (f32[96,1024]{1,0:T(8,128)S(1)}, f32[96,1024]{1,0:T(8,128)S(1)}, u32[]{:S(2)}, u32[]{:S(2)}) collective-permute-start(f32[96,1024]{1,0:T(8,128)S(1)} %mul.1429), channel_id=1, source_target_pairs={{8,0},{10,2},{12,4},{14,6},{0,8},{2,10},{4,12},{6,14},{9,1},{11,3}... | collective-permute-start | bytes 1179656 | tf_op jit(solution)/shard_map/ppermute | solution.py:19
  144.2 2.5 %collective-permute-start.3 = (f32[96,1024]{1,0:T(8,128)S(1)}, f32[96,1024]{1,0:T(8,128)S(1)}, u32[]{:S(2)}, u32[]{:S(2)}) collective-permute-start(f32[96,1024]{1,0:T(8,128)S(1)} %mul.1429), channel_id=1, source_target_pairs={{10,0},{12,2},{14,4},{0,6},{2,8},{4,10},{6,12},{8,14},{11,1},{13,3... | collective-permute-start | bytes 1179656 | tf_op jit(solution)/shard_map/ppermute | solution.py:19
  149.0 29.9 %collective-permute-done.2 = f32[96,1024]{1,0:T(8,128)S(1)} collective-permute-done((f32[96,1024]{1,0:T(8,128)S(1)}, f32[96,1024]{1,0:T(8,128)S(1)}, u32[]{:S(2)}, u32[]{:S(2)}) %collective-permute-start.2) | collective-permute-done | bytes 393248 | tf_op jit(solution)/shard_map/ppermute | solution.py:19
  179.1 17.6 %collective-permute-done.3 = f32[96,1024]{1,0:T(8,128)S(1)} collective-permute-done((f32[96,1024]{1,0:T(8,128)S(1)}, f32[96,1024]{1,0:T(8,128)S(1)}, u32[]{:S(2)}, u32[]{:S(2)}) %collective-permute-start.3) | collective-permute-done | bytes 393248 | tf_op jit(solution)/shard_map/ppermute | solution.py:19
  207.4 2.2 %add_subtract_fusion.6 = (f32[1,1,16,2048]{3,2,1,0:T(8,128)S(1)}, f32[1,1,16,2048]{3,2,1,0:T(8,128)S(1)}, f32[1,1,16,2048]{3,2,1,0:T(8,128)S(1)}, f32[1,1,16,204...) fusion(f32[1,5,16,2048]{3,2,1,0:T(8,128)S(1)} %slice.189, f32[1,8,16,2048]{3,2,1,0:T(8,128)} %copy-done.2, ...), kind=kLoop, calls=%fused_computation.100 | loop fusion | flops 917504 | bytes 2490368 | tf_op jit(solution)/shard_map/sub | solution.py:47
  (108 shorter events, 29.7 us)
Async XLA Ops:
  1.9 53.9 %collective-permute-start = (f32[1,4,16,2048]{3,2,1,0:T(8,128)}, f32[1,4,16,2048]{3,2,1,0:T(8,128)S(1)}, u32[]{:S(2)}, u32[]{:S(2)}) collective-permute-start(f32[1,4,16,2048]{3,2,1,0:T(8,128)} %slice.166), channel_id=1, source_target_pairs={{8,0},{10,2},{12,4},{14,6},{0,8},{2,10},{4,12},{6,14},{9,1},{11,3}... | collective-permute-start | bytes 1572872 | tf_op jit(solution)/shard_map/ppermute | solution.py:19
  8.2 112.6 %collective-permute-start.1 = (f32[1,8,16,2048]{3,2,1,0:T(8,128)}, f32[1,8,16,2048]{3,2,1,0:T(8,128)S(1)}, u32[]{:S(2)}, u32[]{:S(2)}) collective-permute-start(f32[1,8,16,2048]{3,2,1,0:T(8,128)} %slice.171), channel_id=1, source_target_pairs={{8,0},{10,2},{12,4},{14,6},{0,8},{2,10},{4,12},{6,14},{9,1},{11,3}... | collective-permute-start | bytes 3145736 | tf_op jit(solution)/shard_map/ppermute | solution.py:19
  36.9 9.7 %slice-start = ((s8[8388608]{0:T(1024)(128)(4,1)}), s8[4194304]{0:T(1024)(128)(4,1)S(1)}, s32[]{:S(2)}) async-start(s8[8388608]{0:T(1024)(128)(4,1)} %bitcast.145), calls=%async_computation.2 | async-start | bytes 8388608
  36.9 9.7 %slice-start.1 = ((s8[8388608]{0:T(1024)(128)(4,1)}), s8[4194304]{0:T(1024)(128)(4,1)S(1)}, s32[]{:S(2)}) async-start(s8[8388608]{0:T(1024)(128)(4,1)} %bitcast.145), calls=%async_computation.3 | async-start | bytes 8388608
  55.7 11.0 %copy-start.4 = (f32[1,4,16,2048]{3,2,1,0:T(8,128)}, f32[1,4,16,2048]{3,2,1,0:T(8,128)S(1)}, u32[]{:S(2)}) copy-start(f32[1,4,16,2048]{3,2,1,0:T(8,128)S(1)} %collective-permute-done) | copy-start | bytes 1572868
  93.7 9.4 %copy-start = (f32[64,32,512]{2,1,0:T(8,128)S(1)}, f32[64,32,512]{2,1,0:T(8,128)}, u32[]{:S(2)}) copy-start(f32[64,32,512]{2,1,0:T(8,128)} %reshape_reshape.13) | copy-start | bytes 12582916
  112.1 8.8 %copy-start.1 = (f32[64,32,512]{2,1,0:T(8,128)S(1)}, f32[64,32,512]{2,1,0:T(8,128)}, u32[]{:S(2)}) copy-start(f32[64,32,512]{2,1,0:T(8,128)} %fusion.9) | copy-start | bytes 12582916
  120.8 4.0 %copy-start.2 = (f32[1,8,16,2048]{3,2,1,0:T(8,128)}, f32[1,8,16,2048]{3,2,1,0:T(8,128)S(1)}, u32[]{:S(2)}) copy-start(f32[1,8,16,2048]{3,2,1,0:T(8,128)S(1)} %collective-permute-done.1) | copy-start | bytes 3145732
  141.2 37.7 %collective-permute-start.2 = (f32[96,1024]{1,0:T(8,128)S(1)}, f32[96,1024]{1,0:T(8,128)S(1)}, u32[]{:S(2)}, u32[]{:S(2)}) collective-permute-start(f32[96,1024]{1,0:T(8,128)S(1)} %mul.1429), channel_id=1, source_target_pairs={{8,0},{10,2},{12,4},{14,6},{0,8},{2,10},{4,12},{6,14},{9,1},{11,3}... | collective-permute-start | bytes 1179656 | tf_op jit(solution)/shard_map/ppermute | solution.py:19
  144.2 52.5 %collective-permute-start.3 = (f32[96,1024]{1,0:T(8,128)S(1)}, f32[96,1024]{1,0:T(8,128)S(1)}, u32[]{:S(2)}, u32[]{:S(2)}) collective-permute-start(f32[96,1024]{1,0:T(8,128)S(1)} %mul.1429), channel_id=1, source_target_pairs={{10,0},{12,2},{14,4},{0,6},{2,8},{4,10},{6,12},{8,14},{11,1},{13,3... | collective-permute-start | bytes 1179656 | tf_op jit(solution)/shard_map/ppermute | solution.py:19
  146.7 50.2 %collective-permute-start.4 = (f32[96,1024]{1,0:T(8,128)S(1)}, f32[96,1024]{1,0:T(8,128)S(1)}, u32[]{:S(2)}, u32[]{:S(2)}) collective-permute-start(f32[96,1024]{1,0:T(8,128)S(1)} %mul.1429), channel_id=1, source_target_pairs={{12,0},{14,2},{0,4},{2,6},{4,8},{6,10},{8,12},{10,14},{13,1},{15,3... | collective-permute-start | bytes 1179656 | tf_op jit(solution)/shard_map/ppermute | solution.py:19
  146.7 50.4 %collective-permute-start.5 = (f32[96,1024]{1,0:T(8,128)S(1)}, f32[96,1024]{1,0:T(8,128)S(1)}, u32[]{:S(2)}, u32[]{:S(2)}) collective-permute-start(f32[96,1024]{1,0:T(8,128)S(1)} %mul.1429), channel_id=1, source_target_pairs={{14,0},{0,2},{2,4},{4,6},{6,8},{8,10},{10,12},{12,14},{15,1},{1,3}... | collective-permute-start | bytes 1179656 | tf_op jit(solution)/shard_map/ppermute | solution.py:19
  197.4 0.7 copy-start.11
  197.7 0.7 copy-start.10
  202.7 1.4 copy-start.9
  207.4 4.3 %copy-start.5 = (f32[1,4,16,2048]{3,2,1,0:T(8,128)S(1)}, f32[1,4,16,2048]{3,2,1,0:T(8,128)}, u32[]{:S(2)}) copy-start(f32[1,4,16,2048]{3,2,1,0:T(8,128)} %copy-done.4) | copy-start | bytes 1572868
  211.6 1.4 copy-start.3
  211.6 1.4 copy-start.6
  211.6 1.4 copy-start.7
  211.6 1.5 copy-start.8
  213.5 1.1 copy-start.12

commit v3 on v2

--- a/solution.py
+++ b/solution.py
@@ -192,10 +192,13 @@
     retain = retain_row & retain_col & (squared > 0.0)
     safe_sq = jnp.where(retain, squared, 1.0)
     kernel = jnp.where(retain, -2.0 / (safe_sq * norm_factor), 0.0) * weight
-    phi = kernel * spectrum
-    terms = jnp.stack([phi, wave_row * phi, (wave_row * wave_row) * phi])
-    terms = terms.reshape(3, k_count // ray_all, ray_all, 2, m_count, col_count)
-    return jnp.transpose(jnp.sum(terms, axis=(1, 4)), (0, 2, 1, 3))
+    shape = (k_count // ray_all, ray_all, 2, m_count, col_count)
+    spread = spectrum.reshape(shape)
+    sums = [
+        jnp.sum((factor * kernel).reshape(shape[:2] + (1,) + shape[3:]) * spread, axis=(0, 3))
+        for factor in (1.0, wave_row, wave_row * wave_row)
+    ]
+    return jnp.transpose(jnp.stack(sums), (0, 2, 1, 3))
 
 
 def per_device(density, lens_weight, plane_count, ray_state):

time: 220 us -> 229 us (1.041)
  other arithmetic: 36.5 us -> 44.7 us
    sin x8, other arithmetic: 1.45 us -> 4.5 us  [phase_table(): return (jnp.cos(angle), jnp.sin(angle))]
    reduce_sum x1 -> x4, other arithmetic: 7.37 us -> 9.61 us  [folded_spectra(): jnp.sum((factor * kernel).reshape(shape[:2] + (1,) + shape[3:]) * spread,...]
    mul x3 -> x1, other arithmetic: 8.18 us -> 6.99 us  [folded_spectra(): factor * kernel]
    unnamed x38 -> x59, local copies, waits for them, and re-layouts: 11.4 us -> 11.5 us
  transfers between devices with their start and end apart: 6 -> 6, of which waited for: 2 -> 2; matrix products, arithmetic and copies ran while one was open for 48% -> 52% of each run, Pallas kernels for 0% -> 0%
where the time goes in v3:
time: 229 us; the launch traced here: 224 us
  matrix products  58.8 us (26%)
  waiting for transfers between devices  47.5 us (21%)
  local copies, waits for them, and re-layouts  45.1 us (20%)
  other arithmetic  44.7 us (20%)
  blocking collectives  15 us (7%)
  starting transfers between devices  10.7 us (5%)
  between operations  2.53 us (1%)
    dot_general x13, matrix products, mixed(): jnp.einsum(form, left_op, right_op, precision=highest, preferred_element_...  58.8 us
    ppermute x6, waiting for transfers between devices, shifted(): return lax.ppermute(block, axis, route)  47.5 us
    unnamed x59, local copies, waits for them, and re-layouts  11.5 us
    all_to_all x1, blocking collectives, per_device(): lax.all_to_all(rows, 'sky', split_axis=1, concat_axis=0, tiled=True)  10.9 us
    ppermute x6, starting transfers between devices, shifted(): return lax.ppermute(block, axis, route)  10.7 us
    reduce_sum x4, other arithmetic, folded_spectra(): jnp.sum((factor * kernel).reshape(shape[:2] + (1,) + shape[3:]) * spread,...  9.61 us
    another operation x1, local copies, waits for them, and re-layouts, columns_forward(): spread_re.reshape(factor_one, second, col_count)  7.51 us
    another operation x1, local copies, waits for them, and re-layouts, columns_forward(): spread_im.reshape(factor_one, second, col_count)  7.5 us
  transfers between devices with their start and end apart: 6, of which 2 were waited for; matrix products, arithmetic and copies ran while one was open for 52% of the time, Pallas kernels for 0%

profile of v3, /device:TPU:0, one launch (start us, length us, event | category | flops | bytes accessed | tf_op | source)
XLA Modules:
  0.0 224.3 jit_solution(17778832622276697029)
XLA Ops:
  1.1 4.1 %collective-permute-start = (f32[1,4,16,2048]{3,2,1,0:T(8,128)S(1)}, f32[1,4,16,2048]{3,2,1,0:T(8,128)S(1)}, u32[]{:S(2)}, u32[]{:S(2)}) collective-permute-start(f32[1,4,16,2048]{3,2,1,0:T(8,128)S(1)} %slice.166), channel_id=1, source_target_pairs={{8,0},{10,2},{12,4},{14,6},{0,8},{2,10},{4,12},{6,14},{9,1},{11,3}... | collective-permute-start | bytes 1572872 | tf_op jit(solution)/shard_map/ppermute | solution.py:19
  5.2 2.3 %slice.171 = f32[1,8,16,2048]{3,2,1,0:T(8,128)} slice(f32[1,12,16,2048]{3,2,1,0:T(8,128)} %param.7), slice={[0:1], [4:12], [0:16], [0:2048]} | slice | bytes 2097152 | tf_op jit(solution)/shard_map/slice | solution.py:209
  17.0 8.7 %copy.173 = f32[128,8,16,128]{3,2,1,0:T(8,128)} copy(f32[128,8,16,128]{3,1,2,0:T(8,128)} %bitcast.160) | data formatting | bytes 16777216
  27.0 10.2 %convolution_bitcast_fusion = f32[1024,32,128]{2,1,0:T(8,128)S(1)} fusion(f32[1024,16,128]{2,1,0:T(8,128)} %bitcast.150, f32[16,16]{1,0:T(8,128)S(1)} %get-tuple-element.93, f32[16,16]{1,0:T(8,128)S(1)} %get-tuple-element.94), kind=kOutput, calls=%fused_computation | convolution fusion | flops 402653696 | bytes 25167872 | tf_op jit(solution)/shard_map/rvu,vk->rku/dot_general | solution.py:87
  37.2 7.0 %multiply_subtract_fusion = (f32[1024,16,128]{2,1,0:T(8,128)}, f32[1024,16,128]{2,1,0:T(8,128)}) fusion(f32[1024,32,128]{2,1,0:T(8,128)S(1)} %convolution_bitcast_fusion, f32[16,128]{1,0:T(8,128)S(1)} %get-tuple-element.95, f32[16,128]{1,0:T(8,128)S(1)} %get-tuple-element.96), kind=kLoop, calls=%fused_computation.12 | loop fusion | flops 12582912 | bytes 33570816 | tf_op jit(solution)/shard_map/sub | solution.py:121
  44.2 9.6 %fusion.2 = f32[1024,16,128]{2,0,1:T(8,128)S(1)} fusion(f32[1024,16,128]{2,1,0:T(8,128)} %get-tuple-element.59, f32[128,64]{1,0:T(8,128)S(1)} %get-tuple-element.98, f32[128,64]{1,0:T(8,128)} %fusion.112), kind=kOutput, calls=%fused_computation.4 | convolution fusion | flops 1610629120 | bytes 16842752 | tf_op jit(solution)/shard_map/rkj,jn->rkn/dot_general | solution.py:87
  53.9 6.4 %fusion.15 = f32[1024,16,128]{2,0,1:T(8,128)S(1)} fusion(f32[1024,16,128]{2,0,1:T(8,128)S(1)} %fusion.2, f32[1024,16,128]{2,1,0:T(8,128)S(1)} %bitcast.154, f32[128,64]{1,0:T(8,128)} %get-tuple-element.97, f32[128,64]{1,0:T(8,128)S(1)} %get-tuple-element.98), kind=kOutput, calls=%fused_computation.26 | convolution fusion | flops 1612726272 | bytes 25231360 | tf_op jit(solution)/shard_map/rkj,jn->rkn/dot_general | solution.py:87
  60.3 7.0 %broadcast_multiply_fusion = (f32[64,32,512]{2,1,0:T(8,128)}, f32[64,32,512]{2,1,0:T(8,128)}, f32[64,32,512]{2,1,0:T(8,128)}) fusion(f32[64,32]{1,0:T(8,128)} %get-tuple-element.88, f32[512]{0:T(512)} %get-tuple-element.106, f32[64,32]{1,0:T(8,128)} %get-tuple-element.89, f32[512]{0:T(512)} %get-tuple-element.105, pred[512]{0:T(512)(128)(4,1)} %broadcast_compare_fusion, ...), kind=kLoop, calls=%fused_computation.38 | loop fusion | flops 11534336 | bytes 12605952 | tf_op jit(solution)/shard_map/mul | solution.py:198
  67.3 10.9 %all_to_all.27 = f32[1024,16,128]{2,0,1:T(8,128)S(1)} all-to-all(f32[1024,16,128]{2,0,1:T(8,128)S(1)} %fusion.15), channel_id=1, replica_groups=mesh['real'=2,'los'=8,'sky'=2] {'sky'}, dimensions={1} | all-to-all | bytes 16777216 | tf_op jit(solution)/shard_map/all_to_all | solution.py:219
  78.2 4.9 %copy.133 = f32[1024,2,8,128]{3,2,0,1:T(8,128)S(1)} copy(f32[1024,2,8,128]{3,0,2,1:T(8,128)S(1)} %bitcast.155) | data formatting | bytes 16777216 | tf_op jit(solution)/shard_map/all_to_all | solution.py:219
  83.1 7.2 %fusion.219 = (f32[2048,8,64]{2,1,0:T(8,128)}, f32[2048,8,64]{2,1,0:T(8,128)}) fusion(f32[2048,8,128]{2,1,0:T(8,128)S(1)} %bitcast.149), kind=kLoop, calls=%fused_computation.326 | loop fusion | bytes 16777216 | tf_op jit(solution)/shard_map/slice | solution.py:221
  90.2 7.5 %reshape_reshape.14 = f32[64,32,512]{2,1,0:T(8,128)} reshape(f32[2048,8,64]{2,1,0:T(8,128)} %get-tuple-element.63) | data formatting | bytes 8388608 | tf_op jit(solution)/shard_map/reshape;reshape | solution.py:139
  97.7 7.5 %reshape_reshape.13 = f32[64,32,512]{2,1,0:T(8,128)} reshape(f32[2048,8,64]{2,1,0:T(8,128)} %get-tuple-element.62) | data formatting | bytes 8388608 | tf_op jit(solution)/shard_map/reshape;reshape | solution.py:137
  105.2 9.4 %fusion.10 = f32[128,32,512]{2,0,1:T(8,128)S(1)} fusion(f32[64,32,512]{2,1,0:T(8,128)} %reshape_reshape.14, f32[64,64]{1,0:T(8,128)S(1)} %get-tuple-element.99, f32[64,64]{1,0:T(8,128)S(1)} %copy-done.9), kind=kOutput, calls=%fused_computation.19 | convolution fusion | flops 805314560 | bytes 12615680 | tf_op jit(solution)/shard_map/jn,jbc->nbc/dot_general | solution.py:87
  114.7 5.9 %fusion.18 = f32[128,32,512]{2,0,1:T(8,128)S(1)} fusion(f32[128,32,512]{2,0,1:T(8,128)S(1)} %fusion.10, f32[64,32,512]{2,1,0:T(8,128)S(1)} %copy-done, f32[64,64]{1,0:T(8,128)S(1)} %copy-done.8, f32[64,64]{1,0:T(8,128)S(1)} %get-tuple-element.99), kind=kOutput, calls=%fused_computation.27 | convolution fusion | flops 807411712 | bytes 21004288 | tf_op jit(solution)/shard_map/jn,jbc->nbc/dot_general | solution.py:87
  122.8 8.7 %fusion = f32[64,64,512]{2,0,1:T(8,128)S(1)} fusion(f32[64,64,512]{2,0,1:T(8,128)S(1)} %bitcast.151, f32[32,32]{0,1:T(8,128)S(1)} %copy-done.12, f32[32,32]{0,1:T(8,128)S(1)} %copy-done.13, f32[32,32]{0,1:T(8,128)S(1)} %copy-done.11), kind=kOutput, calls=%fused_computation.2 | convolution fusion | flops 805318656 | bytes 16789504 | tf_op jit(solution)/shard_map/kjc,jn->knc/dot_general | solution.py:87
  131.6 9.1 %multiply_reduce_fusion.2 = (f32[64,2,512]{2,1,0:T(2,128)S(1)}, f32[64,2,512]{2,1,0:T(2,128)S(1)}, f32[64,2,512]{2,1,0:T(2,128)S(1)}) fusion(f32[64,2,32,512]{3,2,1,0:T(8,128)S(1)} %bitcast.152, f32[64,32,512]{2,1,0:T(8,128)} %get-tuple-element.87, f32[64,32,512]{2,1,0:T(8,128)} %get-tuple-element.86, f32[64,32,512]{2,1,0:T(8,128)} %get-tuple-element.85), kind=kLoop, calls=%fused_computation.10 | loop fusion | flops 12386304 | bytes 21757952 | tf_op jit(solution)/shard_map/reduce_sum | solution.py:198
  142.5 4.0 %all_to_all.28 = f32[2,1,49152]{2,1,0:T(1,128)S(1)} all-to-all(f32[2,1,49152]{2,1,0:T(1,128)S(1)} %reshape.985), channel_id=1, replica_groups=mesh['real'=2,'los'=8,'sky'=2] {'sky'}, dimensions={0} | all-to-all | bytes 786432 | tf_op jit(solution)/shard_map/all_to_all | solution.py:232
  149.7 3.0 %collective-permute-start.2 = (f32[96,1024]{1,0:T(8,128)S(1)}, f32[96,1024]{1,0:T(8,128)S(1)}, u32[]{:S(2)}, u32[]{:S(2)}) collective-permute-start(f32[96,1024]{1,0:T(8,128)S(1)} %mul.1481), channel_id=1, source_target_pairs={{8,0},{10,2},{12,4},{14,6},{0,8},{2,10},{4,12},{6,14},{9,1},{11,3}... | collective-permute-start | bytes 1179656 | tf_op jit(solution)/shard_map/ppermute | solution.py:19
  152.7 2.5 %collective-permute-start.3 = (f32[96,1024]{1,0:T(8,128)S(1)}, f32[96,1024]{1,0:T(8,128)S(1)}, u32[]{:S(2)}, u32[]{:S(2)}) collective-permute-start(f32[96,1024]{1,0:T(8,128)S(1)} %mul.1481), channel_id=1, source_target_pairs={{10,0},{12,2},{14,4},{0,6},{2,8},{4,10},{6,12},{8,14},{11,1},{13,3... | collective-permute-start | bytes 1179656 | tf_op jit(solution)/shard_map/ppermute | solution.py:19
  157.6 29.9 %collective-permute-done.2 = f32[96,1024]{1,0:T(8,128)S(1)} collective-permute-done((f32[96,1024]{1,0:T(8,128)S(1)}, f32[96,1024]{1,0:T(8,128)S(1)}, u32[]{:S(2)}, u32[]{:S(2)}) %collective-permute-start.2) | collective-permute-done | bytes 393248 | tf_op jit(solution)/shard_map/ppermute | solution.py:19
  187.7 17.6 %collective-permute-done.3 = f32[96,1024]{1,0:T(8,128)S(1)} collective-permute-done((f32[96,1024]{1,0:T(8,128)S(1)}, f32[96,1024]{1,0:T(8,128)S(1)}, u32[]{:S(2)}, u32[]{:S(2)}) %collective-permute-start.3) | collective-permute-done | bytes 393248 | tf_op jit(solution)/shard_map/ppermute | solution.py:19
  215.9 2.2 add_subtract_fusion.6
  218.1 1.9 fusion.55
  (132 shorter events, 34.3 us)
Async XLA Ops:
  1.1 66.2 %collective-permute-start = (f32[1,4,16,2048]{3,2,1,0:T(8,128)S(1)}, f32[1,4,16,2048]{3,2,1,0:T(8,128)S(1)}, u32[]{:S(2)}, u32[]{:S(2)}) collective-permute-start(f32[1,4,16,2048]{3,2,1,0:T(8,128)S(1)} %slice.166), channel_id=1, source_target_pairs={{8,0},{10,2},{12,4},{14,6},{0,8},{2,10},{4,12},{6,14},{9,1},{11,3}... | collective-permute-start | bytes 1572872 | tf_op jit(solution)/shard_map/ppermute | solution.py:19
  7.5 124.1 %collective-permute-start.1 = (f32[1,8,16,2048]{3,2,1,0:T(8,128)}, f32[1,8,16,2048]{3,2,1,0:T(8,128)S(1)}, u32[]{:S(2)}, u32[]{:S(2)}) collective-permute-start(f32[1,8,16,2048]{3,2,1,0:T(8,128)} %slice.171), channel_id=1, source_target_pairs={{8,0},{10,2},{12,4},{14,6},{0,8},{2,10},{4,12},{6,14},{9,1},{11,3}... | collective-permute-start | bytes 3145736 | tf_op jit(solution)/shard_map/ppermute | solution.py:19
  44.2 9.7 %slice-start = ((s8[8388608]{0:T(1024)(128)(4,1)}), s8[4194304]{0:T(1024)(128)(4,1)S(1)}, s32[]{:S(2)}) async-start(s8[8388608]{0:T(1024)(128)(4,1)} %bitcast.153), calls=%async_computation.2 | async-start | bytes 8388608
  44.2 9.7 %slice-start.1 = ((s8[8388608]{0:T(1024)(128)(4,1)}), s8[4194304]{0:T(1024)(128)(4,1)S(1)}, s32[]{:S(2)}) async-start(s8[8388608]{0:T(1024)(128)(4,1)} %bitcast.153), calls=%async_computation.3 | async-start | bytes 8388608
  67.3 10.9 %copy-start.3 = (f32[1,4,16,2048]{3,2,1,0:T(8,128)}, f32[1,4,16,2048]{3,2,1,0:T(8,128)S(1)}, u32[]{:S(2)}) copy-start(f32[1,4,16,2048]{3,2,1,0:T(8,128)S(1)} %collective-permute-done) | copy-start | bytes 1572868
  97.7 7.5 %copy-start.9 = (f32[64,64]{1,0:T(8,128)S(1)}, f32[64,64]{1,0:T(8,128)}, u32[]{:S(2)}) copy-start(f32[64,64]{1,0:T(8,128)} %get-tuple-element.100) | copy-start | bytes 49156
  105.2 9.5 %copy-start = (f32[64,32,512]{2,1,0:T(8,128)S(1)}, f32[64,32,512]{2,1,0:T(8,128)}, u32[]{:S(2)}) copy-start(f32[64,32,512]{2,1,0:T(8,128)} %reshape_reshape.13) | copy-start | bytes 12582916
  105.2 9.5 %copy-start.8 = (f32[64,64]{1,0:T(8,128)S(1)}, f32[64,64]{1,0:T(8,128)}, u32[]{:S(2)}) copy-start(f32[64,64]{1,0:T(8,128)} %fusion.126) | copy-start | bytes 49156
  114.7 5.9 %copy-start.17 = (f32[64,32]{0,1:T(8,128)S(1)}, f32[64,32]{0,1:T(8,128)}, u32[]{:S(2)}) copy-start(f32[64,32]{0,1:T(8,128)} %get-tuple-element.101) | copy-start | bytes 24580
  114.7 5.9 %copy-start.18 = (f32[64,32]{0,1:T(8,128)S(1)}, f32[64,32]{0,1:T(8,128)}, u32[]{:S(2)}) copy-start(f32[64,32]{0,1:T(8,128)} %get-tuple-element.102) | copy-start | bytes 24580
  131.5 9.1 %copy-start.1 = (f32[1,8,16,2048]{3,2,1,0:T(8,128)}, f32[1,8,16,2048]{3,2,1,0:T(8,128)S(1)}, u32[]{:S(2)}) copy-start(f32[1,8,16,2048]{3,2,1,0:T(8,128)S(1)} %collective-permute-done.1) | copy-start | bytes 3145732
  131.6 9.8 %copy-start.14 = (f32[32,32]{0,1:T(8,128)S(1)}, f32[32,32]{0,1:T(8,128)}, u32[]{:S(2)}) copy-start(f32[32,32]{0,1:T(8,128)} %get-tuple-element.107) | copy-start | bytes 12292
  131.6 9.8 %copy-start.15 = (f32[32,32]{0,1:T(8,128)S(1)}, f32[32,32]{0,1:T(8,128)}, u32[]{:S(2)}) copy-start(f32[32,32]{0,1:T(8,128)} %get-tuple-element.108) | copy-start | bytes 12292
  131.6 9.8 %copy-start.16 = (f32[32,32]{0,1:T(8,128)S(1)}, f32[32,32]{0,1:T(8,128)}, u32[]{:S(2)}) copy-start(f32[32,32]{0,1:T(8,128)} %fusion.156) | copy-start | bytes 12292
  149.7 37.7 %collective-permute-start.2 = (f32[96,1024]{1,0:T(8,128)S(1)}, f32[96,1024]{1,0:T(8,128)S(1)}, u32[]{:S(2)}, u32[]{:S(2)}) collective-permute-start(f32[96,1024]{1,0:T(8,128)S(1)} %mul.1481), channel_id=1, source_target_pairs={{8,0},{10,2},{12,4},{14,6},{0,8},{2,10},{4,12},{6,14},{9,1},{11,3}... | collective-permute-start | bytes 1179656 | tf_op jit(solution)/shard_map/ppermute | solution.py:19
  152.7 52.5 %collective-permute-start.3 = (f32[96,1024]{1,0:T(8,128)S(1)}, f32[96,1024]{1,0:T(8,128)S(1)}, u32[]{:S(2)}, u32[]{:S(2)}) collective-permute-start(f32[96,1024]{1,0:T(8,128)S(1)} %mul.1481), channel_id=1, source_target_pairs={{10,0},{12,2},{14,4},{0,6},{2,8},{4,10},{6,12},{8,14},{11,1},{13,3... | collective-permute-start | bytes 1179656 | tf_op jit(solution)/shard_map/ppermute | solution.py:19
  155.3 50.2 %collective-permute-start.4 = (f32[96,1024]{1,0:T(8,128)S(1)}, f32[96,1024]{1,0:T(8,128)S(1)}, u32[]{:S(2)}, u32[]{:S(2)}) collective-permute-start(f32[96,1024]{1,0:T(8,128)S(1)} %mul.1481), channel_id=1, source_target_pairs={{12,0},{14,2},{0,4},{2,6},{4,8},{6,10},{8,12},{10,14},{13,1},{15,3... | collective-permute-start | bytes 1179656 | tf_op jit(solution)/shard_map/ppermute | solution.py:19
  155.3 50.4 %collective-permute-start.5 = (f32[96,1024]{1,0:T(8,128)S(1)}, f32[96,1024]{1,0:T(8,128)S(1)}, u32[]{:S(2)}, u32[]{:S(2)}) collective-permute-start(f32[96,1024]{1,0:T(8,128)S(1)} %mul.1481), channel_id=1, source_target_pairs={{14,0},{0,2},{2,4},{4,6},{6,8},{8,10},{10,12},{12,14},{15,1},{1,3}... | collective-permute-start | bytes 1179656 | tf_op jit(solution)/shard_map/ppermute | solution.py:19
  211.2 1.4 copy-start.10
  215.9 4.2 %copy-start.4 = (f32[1,4,16,2048]{3,2,1,0:T(8,128)S(1)}, f32[1,4,16,2048]{3,2,1,0:T(8,128)}, u32[]{:S(2)}) copy-start(f32[1,4,16,2048]{3,2,1,0:T(8,128)} %copy-done.3) | copy-start | bytes 1572868
  220.1 1.4 copy-start.2
  220.1 1.4 copy-start.5
  220.1 1.4 copy-start.6
  220.2 1.5 copy-start.7
  (6 other events, 5.6 us)

commit v4 on v2

--- a/solution.py
+++ b/solution.py
@@ -113,10 +113,8 @@
     u_idx = jnp.arange(second, dtype=jnp.int32)
     m_idx = jnp.arange(half, dtype=jnp.int32)
     section_re, section_im = phase_table(v_idx, v_idx, first_radix, -1.0)
-    section = jnp.concatenate([section_re, section_im], axis=1)
-    part = mixed("rvu,vk->rku", shaped, section)
-    part_re = part[:, :first_radix]
-    part_im = part[:, first_radix:]
+    part_re = mixed("rvu,vk->rku", shaped, section_re)
+    part_im = mixed("rvu,vk->rku", shaped, section_im)
     twist_re, twist_im = phase_table(v_idx, u_idx, length, -1.0)
     turned_re = part_re * twist_re - part_im * twist_im
     turned_im = part_re * twist_im + part_im * twist_re

time: 220 us -> 217 us (0.986)
  other arithmetic: 36.5 us -> 29.5 us
  matrix products: 58 us -> 64.5 us
  local copies, waits for them, and re-layouts: 45.8 us -> 42.6 us
    sub x1 -> x0, other arithmetic: 7.01 us -> none  [rows_forward(): turned_re = part_re * twist_re - part_im * twist_im]
    dot_general x13 -> x14, matrix products: 58 us -> 64.5 us  [mixed(): jnp.einsum(form, left_op, right_op, precision=highest, preferred_element_...]
    unnamed x38, local copies, waits for them, and re-layouts: 11.4 us -> 8.15 us
  transfers between devices with their start and end apart: 6 -> 6, of which waited for: 2 -> 3; matrix products, arithmetic and copies ran while one was open for 48% -> 47% of each run, Pallas kernels for 0% -> 0%
where the time goes in v4:
time: 217 us; the launch traced here: 212 us
  matrix products  64.5 us (30%)
  waiting for transfers between devices  48.7 us (22%)
  local copies, waits for them, and re-layouts  42.6 us (20%)
  other arithmetic  29.5 us (14%)
  blocking collectives  15 us (7%)
  starting transfers between devices  10 us (5%)
  between operations  2.2 us (1%)
    dot_general x14, matrix products, mixed(): jnp.einsum(form, left_op, right_op, precision=highest, preferred_element_...  64.5 us
    ppermute x6, waiting for transfers between devices, shifted(): return lax.ppermute(block, axis, route)  48.7 us
    all_to_all x1, blocking collectives, per_device(): lax.all_to_all(rows, 'sky', split_axis=1, concat_axis=0, tiled=True)  10.9 us
    ppermute x6, starting transfers between devices, shifted(): return lax.ppermute(block, axis, route)  10 us
    unnamed x38, local copies, waits for them, and re-layouts  8.15 us
    another operation x1, local copies, waits for them, and re-layouts, columns_forward(): spread_im.reshape(factor_one, second, col_count)  7.53 us
    another operation x1, local copies, waits for them, and re-layouts, columns_forward(): spread_re.reshape(factor_one, second, col_count)  7.51 us
    reduce_sum x1, other arithmetic, folded_spectra(): return jnp.transpose(jnp.sum(terms, axis=(1, 4)), (0, 2, 1, 3))  7.37 us
  transfers between devices with their start and end apart: 6, of which 3 were waited for; matrix products, arithmetic and copies ran while one was open for 47% of the time, Pallas kernels for 0%

profile of v4, /device:TPU:0, one launch (start us, length us, event | category | flops | bytes accessed | tf_op | source)
XLA Modules:
  0.0 212.5 jit_solution(7195133602715866516)
XLA Ops:
  1.9 4.0 %collective-permute-start = (f32[1,4,16,2048]{3,2,1,0:T(8,128)}, f32[1,4,16,2048]{3,2,1,0:T(8,128)S(1)}, u32[]{:S(2)}, u32[]{:S(2)}) collective-permute-start(f32[1,4,16,2048]{3,2,1,0:T(8,128)} %slice.160), channel_id=1, source_target_pairs={{8,0},{10,2},{12,4},{14,6},{0,8},{2,10},{4,12},{6,14},{9,1},{11,3}... | collective-permute-start | bytes 1572872 | tf_op jit(solution)/shard_map/ppermute | solution.py:19
  5.9 2.3 %slice.163 = f32[1,8,16,2048]{3,2,1,0:T(8,128)} slice(f32[1,12,16,2048]{3,2,1,0:T(8,128)} %param.7), slice={[0:1], [4:12], [0:16], [0:2048]} | slice | bytes 2097152 | tf_op jit(solution)/shard_map/slice | solution.py:204
  9.7 5.4 %copy.96 = f32[128,8,16,128]{3,2,1,0:T(8,128)S(1)} copy(f32[128,8,16,128]{3,1,2,0:T(8,128)} %bitcast.162) | data formatting | bytes 16777216
  15.0 6.0 %fusion.143 = f32[16,1024,128]{2,0,1:T(8,128)} fusion(f32[1024,16,128]{2,1,0:T(8,128)S(1)} %bitcast.149), kind=kOutput, calls=%fused_computation.239 | convolution fusion | flops 201330176 | bytes 16777216 | tf_op jit(solution)/shard_map/rvu,vk->rku/dot_general | solution.py:87
  22.4 10.8 %subtract_bitcast_fusion = (f32[1024,16,128]{2,1,0:T(8,128)}, f32[1024,16,128]{2,1,0:T(8,128)}) fusion(f32[16,1024,128]{2,0,1:T(8,128)} %fusion.143, f32[16,128]{1,0:T(8,128)S(1)} %get-tuple-element.89, f32[16,128]{1,0:T(8,128)S(1)} %get-tuple-element.90, f32[1024,16,128]{2,1,0:T(8,128)S(1)} %bitcast.150), kind=kOutput, calls=%fused_computation.9 | convolution fusion | flops 213913088 | bytes 33570816 | tf_op jit(solution)/shard_map/rvu,vk->rku/dot_general | solution.py:87
  33.2 9.6 %fusion.2 = f32[1024,16,128]{2,0,1:T(8,128)S(1)} fusion(f32[1024,16,128]{2,1,0:T(8,128)} %get-tuple-element.58, f32[128,64]{1,0:T(8,128)S(1)} %get-tuple-element.92, f32[128,64]{1,0:T(8,128)S(1)} %fusion.113), kind=kOutput, calls=%fused_computation.4 | convolution fusion | flops 1610629120 | bytes 16842752 | tf_op jit(solution)/shard_map/rkj,jn->rkn/dot_general | solution.py:87
  42.9 5.6 %fusion.15 = f32[1024,16,128]{2,0,1:T(8,128)S(1)} fusion(f32[1024,16,128]{2,0,1:T(8,128)S(1)} %fusion.2, f32[1024,16,128]{2,1,0:T(8,128)S(1)} %bitcast.155, f32[128,64]{1,0:T(8,128)S(1)} %get-tuple-element.91, f32[128,64]{1,0:T(8,128)S(1)} %get-tuple-element.92), kind=kOutput, calls=%fused_computation.26 | convolution fusion | flops 1612726272 | bytes 25231360 | tf_op jit(solution)/shard_map/rkj,jn->rkn/dot_general | solution.py:87
  48.4 3.6 %fusion.9 = f32[64,32,512]{2,1,0:T(8,128)} fusion(f32[512]{0:T(512)S(1)} %get-tuple-element.100, f32[64,32]{1,0:T(8,128)S(1)} %get-tuple-element.87, f32[512]{0:T(512)S(1)} %get-tuple-element.99, pred[512]{0:T(512)(128)(4,1)S(1)} %broadcast_compare_fusion, pred[64,32]{1,0:T(8,128)(4,1)S(1)} %fusion.108), kind=kLoop, calls=%fused_computation.15 | loop fusion | flops 9437184 | bytes 4209152 | tf_op jit(solution)/shard_map/mul | solution.py:192
  52.6 10.9 %all_to_all.27 = f32[1024,16,128]{2,0,1:T(8,128)S(1)} all-to-all(f32[1024,16,128]{2,0,1:T(8,128)S(1)} %fusion.15), channel_id=1, replica_groups=mesh['real'=2,'los'=8,'sky'=2] {'sky'}, dimensions={1} | all-to-all | bytes 16777216 | tf_op jit(solution)/shard_map/all_to_all | solution.py:214
  63.5 4.9 %copy.76 = f32[1024,2,8,128]{3,2,0,1:T(8,128)S(1)} copy(f32[1024,2,8,128]{3,0,2,1:T(8,128)S(1)} %bitcast.157) | data formatting | bytes 16777216 | tf_op jit(solution)/shard_map/all_to_all | solution.py:214
  68.4 7.2 %fusion.237 = (f32[2048,8,64]{2,1,0:T(8,128)}, f32[2048,8,64]{2,1,0:T(8,128)}) fusion(f32[2048,8,128]{2,1,0:T(8,128)S(1)} %bitcast.148), kind=kLoop, calls=%fused_computation.331 | loop fusion | bytes 16777216 | tf_op jit(solution)/shard_map/slice | solution.py:216
  75.5 7.5 %reshape_reshape.14 = f32[64,32,512]{2,1,0:T(8,128)} reshape(f32[2048,8,64]{2,1,0:T(8,128)} %get-tuple-element.62) | data formatting | bytes 8388608 | tf_op jit(solution)/shard_map/reshape;reshape | solution.py:137
  83.0 7.5 %reshape_reshape.13 = f32[64,32,512]{2,1,0:T(8,128)} reshape(f32[2048,8,64]{2,1,0:T(8,128)} %get-tuple-element.61) | data formatting | bytes 8388608 | tf_op jit(solution)/shard_map/reshape;reshape | solution.py:135
  90.5 9.4 %fusion.10 = f32[128,32,512]{2,0,1:T(8,128)S(1)} fusion(f32[64,32,512]{2,1,0:T(8,128)} %reshape_reshape.14, f32[64,64]{1,0:T(8,128)S(1)} %get-tuple-element.93, f32[64,64]{1,0:T(8,128)S(1)} %get-tuple-element.94), kind=kOutput, calls=%fused_computation.16 | convolution fusion | flops 805314560 | bytes 12615680 | tf_op jit(solution)/shard_map/jn,jbc->nbc/dot_general | solution.py:87
  100.0 5.9 %fusion.18 = f32[128,32,512]{2,0,1:T(8,128)S(1)} fusion(f32[128,32,512]{2,0,1:T(8,128)S(1)} %fusion.10, f32[64,32,512]{2,1,0:T(8,128)S(1)} %copy-done, f32[64,64]{1,0:T(8,128)S(1)} %fusion.127, f32[64,64]{1,0:T(8,128)S(1)} %get-tuple-element.93), kind=kOutput, calls=%fused_computation.27 | convolution fusion | flops 807411712 | bytes 21004288 | tf_op jit(solution)/shard_map/jn,jbc->nbc/dot_general | solution.py:87
  108.9 8.7 %fusion = f32[64,64,512]{2,0,1:T(8,128)S(1)} fusion(f32[64,64,512]{2,0,1:T(8,128)S(1)} %bitcast.152, f32[32,32]{0,1:T(8,128)S(1)} %get-tuple-element.98, f32[32,32]{0,1:T(8,128)S(1)} %fusion.164, f32[32,32]{0,1:T(8,128)S(1)} %get-tuple-element.97), kind=kOutput, calls=%fused_computation.2 | convolution fusion | flops 805318656 | bytes 16789504 | tf_op jit(solution)/shard_map/kjc,jn->knc/dot_general | solution.py:87
  117.6 4.0 %broadcast_multiply_fusion.1 = (f32[64,2,32,512]{3,2,1,0:T(8,128)}, f32[64,2,32,512]{3,2,1,0:T(8,128)S(1)}) fusion(f32[64,32]{1,0:T(8,128)S(1)} %get-tuple-element.88, f32[64,2,32,512]{3,2,1,0:T(8,128)S(1)} %bitcast.153, f32[64,32,512]{2,1,0:T(8,128)S(1)} %copy-done.1), kind=kLoop, calls=%fused_computation.21 | loop fusion | flops 4194304 | bytes 29368320 | tf_op jit(solution)/shard_map/mul | solution.py:194
  122.3 7.4 %maximum_reduce_fusion = f32[3,32,2,512]{3,2,1,0:T(2,128)S(1)} fusion(f32[1,2,32,2,32,512]{5,4,3,2,1,0:T(8,128)S(1)} %bitcast.151, f32[1,2,32,2,32,512]{5,4,3,2,1,0:T(8,128)} %bitcast.156, f32[1,2,32,2,32,512]{5,4,3,2,1,0:T(8,128)S(1)} %bitcast.147), kind=kLoop, calls=%fused_computation | loop fusion | flops 18776064 | bytes 25559040 | tf_op jit(solution)/shard_map/reduce_sum | solution.py:196
  130.8 4.0 %all_to_all.28 = f32[2,1,49152]{2,1,0:T(1,128)S(1)} all-to-all(f32[2,1,49152]{2,1,0:T(1,128)S(1)} %reshape.942), channel_id=1, replica_groups=mesh['real'=2,'los'=8,'sky'=2] {'sky'}, dimensions={0} | all-to-all | bytes 786432 | tf_op jit(solution)/shard_map/all_to_all | solution.py:227
  138.2 2.4 %collective-permute-start.2 = (f32[96,1024]{1,0:T(8,128)S(1)}, f32[96,1024]{1,0:T(8,128)S(1)}, u32[]{:S(2)}, u32[]{:S(2)}) collective-permute-start(f32[96,1024]{1,0:T(8,128)S(1)} %mul.1433), channel_id=1, source_target_pairs={{8,0},{10,2},{12,4},{14,6},{0,8},{2,10},{4,12},{6,14},{9,1},{11,3}... | collective-permute-start | bytes 1179656 | tf_op jit(solution)/shard_map/ppermute | solution.py:19
  140.6 2.5 %collective-permute-start.3 = (f32[96,1024]{1,0:T(8,128)S(1)}, f32[96,1024]{1,0:T(8,128)S(1)}, u32[]{:S(2)}, u32[]{:S(2)}) collective-permute-start(f32[96,1024]{1,0:T(8,128)S(1)} %mul.1433), channel_id=1, source_target_pairs={{10,0},{12,2},{14,4},{0,6},{2,8},{4,10},{6,12},{8,14},{11,1},{13,3... | collective-permute-start | bytes 1179656 | tf_op jit(solution)/shard_map/ppermute | solution.py:19
  145.4 30.2 %collective-permute-done.2 = f32[96,1024]{1,0:T(8,128)S(1)} collective-permute-done((f32[96,1024]{1,0:T(8,128)S(1)}, f32[96,1024]{1,0:T(8,128)S(1)}, u32[]{:S(2)}, u32[]{:S(2)}) %collective-permute-start.2) | collective-permute-done | bytes 393248 | tf_op jit(solution)/shard_map/ppermute | solution.py:19
  175.8 17.9 %collective-permute-done.3 = f32[96,1024]{1,0:T(8,128)S(1)} collective-permute-done((f32[96,1024]{1,0:T(8,128)S(1)}, f32[96,1024]{1,0:T(8,128)S(1)}, u32[]{:S(2)}, u32[]{:S(2)}) %collective-permute-start.3) | collective-permute-done | bytes 393248 | tf_op jit(solution)/shard_map/ppermute | solution.py:19
  204.3 2.2 %add_subtract_fusion.6 = (f32[1,1,16,2048]{3,2,1,0:T(8,128)S(1)}, f32[1,1,16,2048]{3,2,1,0:T(8,128)S(1)}, f32[1,1,16,2048]{3,2,1,0:T(8,128)S(1)}, f32[1,1,16,204...) fusion(f32[1,5,16,2048]{3,2,1,0:T(8,128)S(1)} %slice.181, f32[1,8,16,2048]{3,2,1,0:T(8,128)} %copy-done.2, ...), kind=kLoop, calls=%fused_computation.99 | loop fusion | flops 917504 | bytes 2490368 | tf_op jit(solution)/shard_map/sub | solution.py:47
  (107 shorter events, 30.3 us)
Async XLA Ops:
  1.9 50.7 %collective-permute-start = (f32[1,4,16,2048]{3,2,1,0:T(8,128)}, f32[1,4,16,2048]{3,2,1,0:T(8,128)S(1)}, u32[]{:S(2)}, u32[]{:S(2)}) collective-permute-start(f32[1,4,16,2048]{3,2,1,0:T(8,128)} %slice.160), channel_id=1, source_target_pairs={{8,0},{10,2},{12,4},{14,6},{0,8},{2,10},{4,12},{6,14},{9,1},{11,3}... | collective-permute-start | bytes 1572872 | tf_op jit(solution)/shard_map/ppermute | solution.py:19
  8.2 109.4 %collective-permute-start.1 = (f32[1,8,16,2048]{3,2,1,0:T(8,128)}, f32[1,8,16,2048]{3,2,1,0:T(8,128)S(1)}, u32[]{:S(2)}, u32[]{:S(2)}) collective-permute-start(f32[1,8,16,2048]{3,2,1,0:T(8,128)} %slice.163), channel_id=1, source_target_pairs={{8,0},{10,2},{12,4},{14,6},{0,8},{2,10},{4,12},{6,14},{9,1},{11,3}... | collective-permute-start | bytes 3145736 | tf_op jit(solution)/shard_map/ppermute | solution.py:19
  33.2 9.6 %slice-start = ((s8[8388608]{0:T(1024)(128)(4,1)}), s8[4194304]{0:T(1024)(128)(4,1)S(1)}, s32[]{:S(2)}) async-start(s8[8388608]{0:T(1024)(128)(4,1)} %bitcast.154), calls=%async_computation.2 | async-start | bytes 8388608
  33.2 9.6 %slice-start.1 = ((s8[8388608]{0:T(1024)(128)(4,1)}), s8[4194304]{0:T(1024)(128)(4,1)S(1)}, s32[]{:S(2)}) async-start(s8[8388608]{0:T(1024)(128)(4,1)} %bitcast.154), calls=%async_computation.3 | async-start | bytes 8388608
  52.6 10.9 %copy-start.4 = (f32[1,4,16,2048]{3,2,1,0:T(8,128)}, f32[1,4,16,2048]{3,2,1,0:T(8,128)S(1)}, u32[]{:S(2)}) copy-start(f32[1,4,16,2048]{3,2,1,0:T(8,128)S(1)} %collective-permute-done) | copy-start | bytes 1572868
  90.5 9.4 %copy-start = (f32[64,32,512]{2,1,0:T(8,128)S(1)}, f32[64,32,512]{2,1,0:T(8,128)}, u32[]{:S(2)}) copy-start(f32[64,32,512]{2,1,0:T(8,128)} %reshape_reshape.13) | copy-start | bytes 12582916
  108.9 8.8 %copy-start.1 = (f32[64,32,512]{2,1,0:T(8,128)S(1)}, f32[64,32,512]{2,1,0:T(8,128)}, u32[]{:S(2)}) copy-start(f32[64,32,512]{2,1,0:T(8,128)} %fusion.9) | copy-start | bytes 12582916
  117.6 4.0 %copy-start.2 = (f32[1,8,16,2048]{3,2,1,0:T(8,128)}, f32[1,8,16,2048]{3,2,1,0:T(8,128)S(1)}, u32[]{:S(2)}) copy-start(f32[1,8,16,2048]{3,2,1,0:T(8,128)S(1)} %collective-permute-done.1) | copy-start | bytes 3145732
  138.2 37.4 %collective-permute-start.2 = (f32[96,1024]{1,0:T(8,128)S(1)}, f32[96,1024]{1,0:T(8,128)S(1)}, u32[]{:S(2)}, u32[]{:S(2)}) collective-permute-start(f32[96,1024]{1,0:T(8,128)S(1)} %mul.1433), channel_id=1, source_target_pairs={{8,0},{10,2},{12,4},{14,6},{0,8},{2,10},{4,12},{6,14},{9,1},{11,3}... | collective-permute-start | bytes 1179656 | tf_op jit(solution)/shard_map/ppermute | solution.py:19
  140.6 53.2 %collective-permute-start.3 = (f32[96,1024]{1,0:T(8,128)S(1)}, f32[96,1024]{1,0:T(8,128)S(1)}, u32[]{:S(2)}, u32[]{:S(2)}) collective-permute-start(f32[96,1024]{1,0:T(8,128)S(1)} %mul.1433), channel_id=1, source_target_pairs={{10,0},{12,2},{14,4},{0,6},{2,8},{4,10},{6,12},{8,14},{11,1},{13,3... | collective-permute-start | bytes 1179656 | tf_op jit(solution)/shard_map/ppermute | solution.py:19
  143.1 50.8 %collective-permute-start.4 = (f32[96,1024]{1,0:T(8,128)S(1)}, f32[96,1024]{1,0:T(8,128)S(1)}, u32[]{:S(2)}, u32[]{:S(2)}) collective-permute-start(f32[96,1024]{1,0:T(8,128)S(1)} %mul.1433), channel_id=1, source_target_pairs={{12,0},{14,2},{0,4},{2,6},{4,8},{6,10},{8,12},{10,14},{13,1},{15,3... | collective-permute-start | bytes 1179656 | tf_op jit(solution)/shard_map/ppermute | solution.py:19
  143.1 51.1 %collective-permute-start.5 = (f32[96,1024]{1,0:T(8,128)S(1)}, f32[96,1024]{1,0:T(8,128)S(1)}, u32[]{:S(2)}, u32[]{:S(2)}) collective-permute-start(f32[96,1024]{1,0:T(8,128)S(1)} %mul.1433), channel_id=1, source_target_pairs={{14,0},{0,2},{2,4},{4,6},{6,8},{8,10},{10,12},{12,14},{15,1},{1,3}... | collective-permute-start | bytes 1179656 | tf_op jit(solution)/shard_map/ppermute | solution.py:19
  194.4 0.7 copy-start.11
  194.7 0.7 copy-start.10
  199.7 1.4 copy-start.9
  204.3 4.3 %copy-start.5 = (f32[1,4,16,2048]{3,2,1,0:T(8,128)S(1)}, f32[1,4,16,2048]{3,2,1,0:T(8,128)}, u32[]{:S(2)}) copy-start(f32[1,4,16,2048]{3,2,1,0:T(8,128)} %copy-done.4) | copy-start | bytes 1572868
  208.5 1.4 copy-start.3
  208.5 1.4 copy-start.6
  208.5 1.4 copy-start.7
  208.5 1.5 copy-start.8
  210.4 1.1 copy-start.12

commit v5 on v4

--- a/solution.py
+++ b/solution.py
@@ -222,7 +222,9 @@
     folds = folded_spectra(spectrum, col_idx, ray_all)
     q_idx = jnp.arange(ray_all, dtype=jnp.int32)
     back = block_table(q_idx, q_idx, ray_all, 1.0)
-    at_rows = mixed("pjc,jn->pnc", folds.reshape(3, 2 * ray_all, k_local * half), back)
+    at_rows = mixed("pjc,jn->pnc", folds[:, 0], back[:ray_all]) + mixed(
+        "pjc,jn->pnc", folds[:, 1], back[ray_all:]
+    )
     at_rows = at_rows.reshape(3, 2, ray_all, k_local, half)
     returned = lax.all_to_all(at_rows, "sky", split_axis=2, concat_axis=3, tiled=True)
     k_all = returned.shape[3]

time: 217 us -> 217 us (level)
    dot_general x14 -> x15, matrix products: 64.5 us -> 64.8 us  [mixed(): jnp.einsum(form, left_op, right_op, precision=highest, preferred_element_...]
where the time goes in v5:
time: 217 us; the launch traced here: 213 us
  matrix products  64.8 us (30%)
  waiting for transfers between devices  48.8 us (22%)
  local copies, waits for them, and re-layouts  42.6 us (20%)
  other arithmetic  29.7 us (14%)
  blocking collectives  15 us (7%)
  starting transfers between devices  9.89 us (5%)
  between operations  2.36 us (1%)
    dot_general x15, matrix products, mixed(): jnp.einsum(form, left_op, right_op, precision=highest, preferred_element_...  64.8 us
    ppermute x6, waiting for transfers between devices, shifted(): return lax.ppermute(block, axis, route)  48.8 us
    all_to_all x1, blocking collectives, per_device(): lax.all_to_all(rows, 'sky', split_axis=1, concat_axis=0, tiled=True)  10.9 us
    ppermute x6, starting transfers between devices, shifted(): return lax.ppermute(block, axis, route)  9.89 us
    unnamed x38, local copies, waits for them, and re-layouts  8.15 us
    reduce_sum x1, other arithmetic, folded_spectra(): return jnp.transpose(jnp.sum(terms, axis=(1, 4)), (0, 2, 1, 3))  7.58 us
    another operation x1, local copies, waits for them, and re-layouts, columns_forward(): spread_im.reshape(factor_one, second, col_count)  7.53 us
    another operation x1, local copies, waits for them, and re-layouts, columns_forward(): spread_re.reshape(factor_one, second, col_count)  7.51 us
  transfers between devices with their start and end apart: 6, of which 3 were waited for; matrix products, arithmetic and copies ran while one was open for 47% of the time, Pallas kernels for 0%

profile of v5, /device:TPU:0, one launch (start us, length us, event | category | flops | bytes accessed | tf_op | source)
XLA Modules:
  0.0 213.1 jit_solution(5461307119286452510)
XLA Ops:
  1.9 4.0 %collective-permute-start = (f32[1,4,16,2048]{3,2,1,0:T(8,128)}, f32[1,4,16,2048]{3,2,1,0:T(8,128)S(1)}, u32[]{:S(2)}, u32[]{:S(2)}) collective-permute-start(f32[1,4,16,2048]{3,2,1,0:T(8,128)} %slice.166), channel_id=1, source_target_pairs={{8,0},{10,2},{12,4},{14,6},{0,8},{2,10},{4,12},{6,14},{9,1},{11,3}... | collective-permute-start | bytes 1572872 | tf_op jit(solution)/shard_map/ppermute | solution.py:19
  5.9 2.3 %slice.169 = f32[1,8,16,2048]{3,2,1,0:T(8,128)} slice(f32[1,12,16,2048]{3,2,1,0:T(8,128)} %param.7), slice={[0:1], [4:12], [0:16], [0:2048]} | slice | bytes 2097152 | tf_op jit(solution)/shard_map/slice | solution.py:204
  9.7 5.4 %copy.87 = f32[128,8,16,128]{3,2,1,0:T(8,128)S(1)} copy(f32[128,8,16,128]{3,1,2,0:T(8,128)} %bitcast.171) | data formatting | bytes 16777216
  15.0 6.1 %fusion.143 = f32[16,1024,128]{2,0,1:T(8,128)} fusion(f32[1024,16,128]{2,1,0:T(8,128)S(1)} %bitcast.158), kind=kOutput, calls=%fused_computation.243 | convolution fusion | flops 201330176 | bytes 16777216 | tf_op jit(solution)/shard_map/rvu,vk->rku/dot_general | solution.py:87
  22.4 10.8 %subtract_bitcast_fusion = (f32[1024,16,128]{2,1,0:T(8,128)}, f32[1024,16,128]{2,1,0:T(8,128)}) fusion(f32[16,1024,128]{2,0,1:T(8,128)} %fusion.143, f32[16,128]{1,0:T(8,128)S(1)} %get-tuple-element.89, f32[16,128]{1,0:T(8,128)S(1)} %get-tuple-element.90, f32[1024,16,128]{2,1,0:T(8,128)S(1)} %bitcast.159), kind=kOutput, calls=%fused_computation.9 | convolution fusion | flops 213913088 | bytes 33570816 | tf_op jit(solution)/shard_map/rvu,vk->rku/dot_general | solution.py:87
  33.2 9.6 %fusion.2 = f32[1024,16,128]{2,0,1:T(8,128)S(1)} fusion(f32[1024,16,128]{2,1,0:T(8,128)} %get-tuple-element.58, f32[128,64]{1,0:T(8,128)S(1)} %get-tuple-element.92, f32[128,64]{1,0:T(8,128)S(1)} %fusion.113), kind=kOutput, calls=%fused_computation.4 | convolution fusion | flops 1610629120 | bytes 16842752 | tf_op jit(solution)/shard_map/rkj,jn->rkn/dot_general | solution.py:87
  42.9 5.6 %fusion.15 = f32[1024,16,128]{2,0,1:T(8,128)S(1)} fusion(f32[1024,16,128]{2,0,1:T(8,128)S(1)} %fusion.2, f32[1024,16,128]{2,1,0:T(8,128)S(1)} %bitcast.164, f32[128,64]{1,0:T(8,128)S(1)} %get-tuple-element.91, f32[128,64]{1,0:T(8,128)S(1)} %get-tuple-element.92), kind=kOutput, calls=%fused_computation.26 | convolution fusion | flops 1612726272 | bytes 25231360 | tf_op jit(solution)/shard_map/rkj,jn->rkn/dot_general | solution.py:87
  48.5 3.6 %fusion.9 = f32[64,32,512]{2,1,0:T(8,128)} fusion(f32[512]{0:T(512)S(1)} %get-tuple-element.100, f32[64,32]{1,0:T(8,128)S(1)} %get-tuple-element.87, f32[512]{0:T(512)S(1)} %get-tuple-element.99, pred[512]{0:T(512)(128)(4,1)S(1)} %broadcast_compare_fusion, pred[64,32]{1,0:T(8,128)(4,1)S(1)} %fusion.108), kind=kLoop, calls=%fused_computation.15 | loop fusion | flops 9437184 | bytes 4209152 | tf_op jit(solution)/shard_map/mul | solution.py:192
  52.6 10.9 %all_to_all.27 = f32[1024,16,128]{2,0,1:T(8,128)S(1)} all-to-all(f32[1024,16,128]{2,0,1:T(8,128)S(1)} %fusion.15), channel_id=1, replica_groups=mesh['real'=2,'los'=8,'sky'=2] {'sky'}, dimensions={1} | all-to-all | bytes 16777216 | tf_op jit(solution)/shard_map/all_to_all | solution.py:214
  63.5 4.9 %copy.61 = f32[1024,2,8,128]{3,2,0,1:T(8,128)S(1)} copy(f32[1024,2,8,128]{3,0,2,1:T(8,128)S(1)} %bitcast.166) | data formatting | bytes 16777216 | tf_op jit(solution)/shard_map/all_to_all | solution.py:214
  68.4 7.2 %fusion.238 = (f32[2048,8,64]{2,1,0:T(8,128)}, f32[2048,8,64]{2,1,0:T(8,128)}) fusion(f32[2048,8,128]{2,1,0:T(8,128)S(1)} %bitcast.157), kind=kLoop, calls=%fused_computation.336 | loop fusion | bytes 16777216 | tf_op jit(solution)/shard_map/slice | solution.py:216
  75.5 7.5 %reshape_reshape.14 = f32[64,32,512]{2,1,0:T(8,128)} reshape(f32[2048,8,64]{2,1,0:T(8,128)} %get-tuple-element.62) | data formatting | bytes 8388608 | tf_op jit(solution)/shard_map/reshape;reshape | solution.py:137
  83.0 7.5 %reshape_reshape.13 = f32[64,32,512]{2,1,0:T(8,128)} reshape(f32[2048,8,64]{2,1,0:T(8,128)} %get-tuple-element.61) | data formatting | bytes 8388608 | tf_op jit(solution)/shard_map/reshape;reshape | solution.py:135
  90.5 9.4 %fusion.10 = f32[128,32,512]{2,0,1:T(8,128)S(1)} fusion(f32[64,32,512]{2,1,0:T(8,128)} %reshape_reshape.14, f32[64,64]{1,0:T(8,128)S(1)} %get-tuple-element.93, f32[64,64]{1,0:T(8,128)S(1)} %get-tuple-element.94), kind=kOutput, calls=%fused_computation.16 | convolution fusion | flops 805314560 | bytes 12615680 | tf_op jit(solution)/shard_map/jn,jbc->nbc/dot_general | solution.py:87
  100.0 5.9 %fusion.18 = f32[128,32,512]{2,0,1:T(8,128)S(1)} fusion(f32[128,32,512]{2,0,1:T(8,128)S(1)} %fusion.10, f32[64,32,512]{2,1,0:T(8,128)S(1)} %copy-done, f32[64,64]{1,0:T(8,128)S(1)} %fusion.127, f32[64,64]{1,0:T(8,128)S(1)} %get-tuple-element.93), kind=kOutput, calls=%fused_computation.27 | convolution fusion | flops 807411712 | bytes 21004288 | tf_op jit(solution)/shard_map/jn,jbc->nbc/dot_general | solution.py:87
  108.9 8.7 %fusion = f32[64,64,512]{2,0,1:T(8,128)S(1)} fusion(f32[64,64,512]{2,0,1:T(8,128)S(1)} %bitcast.161, f32[32,32]{0,1:T(8,128)S(1)} %get-tuple-element.98, f32[32,32]{0,1:T(8,128)S(1)} %fusion.164, f32[32,32]{0,1:T(8,128)S(1)} %get-tuple-element.97), kind=kOutput, calls=%fused_computation.2 | convolution fusion | flops 805318656 | bytes 16789504 | tf_op jit(solution)/shard_map/kjc,jn->knc/dot_general | solution.py:87
  117.6 4.0 %broadcast_multiply_fusion.1 = (f32[64,2,32,512]{3,2,1,0:T(8,128)}, f32[64,2,32,512]{3,2,1,0:T(8,128)S(1)}) fusion(f32[64,32]{1,0:T(8,128)S(1)} %get-tuple-element.88, f32[64,2,32,512]{3,2,1,0:T(8,128)S(1)} %bitcast.162, f32[64,32,512]{2,1,0:T(8,128)S(1)} %copy-done.1), kind=kLoop, calls=%fused_computation.21 | loop fusion | flops 4194304 | bytes 29368320 | tf_op jit(solution)/shard_map/mul | solution.py:194
  122.3 7.6 %maximum_reduce_fusion = f32[3,32,2,512]{3,2,1,0:T(2,128)S(1)} fusion(f32[1,2,32,2,32,512]{5,4,3,2,1,0:T(8,128)S(1)} %bitcast.160, f32[1,2,32,2,32,512]{5,4,3,2,1,0:T(8,128)} %bitcast.165, f32[1,2,32,2,32,512]{5,4,3,2,1,0:T(8,128)S(1)} %bitcast.156), kind=kLoop, calls=%fused_computation | loop fusion | flops 18776064 | bytes 25559040 | tf_op jit(solution)/shard_map/reduce_sum | solution.py:196
  131.3 4.0 %all_to_all.28 = f32[2,1,49152]{2,1,0:T(1,128)S(1)} all-to-all(f32[2,1,49152]{2,1,0:T(1,128)S(1)} %reshape.939), channel_id=1, replica_groups=mesh['real'=2,'los'=8,'sky'=2] {'sky'}, dimensions={0} | all-to-all | bytes 786432 | tf_op jit(solution)/shard_map/all_to_all | solution.py:229
  138.6 2.5 %collective-permute-start.2 = (f32[96,1024]{1,0:T(8,128)S(1)}, f32[96,1024]{1,0:T(8,128)S(1)}, u32[]{:S(2)}, u32[]{:S(2)}) collective-permute-start(f32[96,1024]{1,0:T(8,128)S(1)} %mul.1433), channel_id=1, source_target_pairs={{8,0},{10,2},{12,4},{14,6},{0,8},{2,10},{4,12},{6,14},{9,1},{11,3}... | collective-permute-start | bytes 1179656 | tf_op jit(solution)/shard_map/ppermute | solution.py:19
  141.1 2.5 %collective-permute-start.3 = (f32[96,1024]{1,0:T(8,128)S(1)}, f32[96,1024]{1,0:T(8,128)S(1)}, u32[]{:S(2)}, u32[]{:S(2)}) collective-permute-start(f32[96,1024]{1,0:T(8,128)S(1)} %mul.1433), channel_id=1, source_target_pairs={{10,0},{12,2},{14,4},{0,6},{2,8},{4,10},{6,12},{8,14},{11,1},{13,3... | collective-permute-start | bytes 1179656 | tf_op jit(solution)/shard_map/ppermute | solution.py:19
  145.8 30.3 %collective-permute-done.2 = f32[96,1024]{1,0:T(8,128)S(1)} collective-permute-done((f32[96,1024]{1,0:T(8,128)S(1)}, f32[96,1024]{1,0:T(8,128)S(1)}, u32[]{:S(2)}, u32[]{:S(2)}) %collective-permute-start.2) | collective-permute-done | bytes 393248 | tf_op jit(solution)/shard_map/ppermute | solution.py:19
  176.3 17.9 %collective-permute-done.3 = f32[96,1024]{1,0:T(8,128)S(1)} collective-permute-done((f32[96,1024]{1,0:T(8,128)S(1)}, f32[96,1024]{1,0:T(8,128)S(1)}, u32[]{:S(2)}, u32[]{:S(2)}) %collective-permute-start.3) | collective-permute-done | bytes 393248 | tf_op jit(solution)/shard_map/ppermute | solution.py:19
  204.8 2.2 %add_subtract_fusion.6 = (f32[1,1,16,2048]{3,2,1,0:T(8,128)S(1)}, f32[1,1,16,2048]{3,2,1,0:T(8,128)S(1)}, f32[1,1,16,2048]{3,2,1,0:T(8,128)S(1)}, f32[1,1,16,204...) fusion(f32[1,5,16,2048]{3,2,1,0:T(8,128)S(1)} %slice.189, f32[1,8,16,2048]{3,2,1,0:T(8,128)} %copy-done.2, ...), kind=kLoop, calls=%fused_computation.104 | loop fusion | flops 917504 | bytes 2490368 | tf_op jit(solution)/shard_map/sub | solution.py:47
  (108 shorter events, 30.3 us)
Async XLA Ops:
  1.9 50.7 %collective-permute-start = (f32[1,4,16,2048]{3,2,1,0:T(8,128)}, f32[1,4,16,2048]{3,2,1,0:T(8,128)S(1)}, u32[]{:S(2)}, u32[]{:S(2)}) collective-permute-start(f32[1,4,16,2048]{3,2,1,0:T(8,128)} %slice.166), channel_id=1, source_target_pairs={{8,0},{10,2},{12,4},{14,6},{0,8},{2,10},{4,12},{6,14},{9,1},{11,3}... | collective-permute-start | bytes 1572872 | tf_op jit(solution)/shard_map/ppermute | solution.py:19
  8.2 109.4 %collective-permute-start.1 = (f32[1,8,16,2048]{3,2,1,0:T(8,128)}, f32[1,8,16,2048]{3,2,1,0:T(8,128)S(1)}, u32[]{:S(2)}, u32[]{:S(2)}) collective-permute-start(f32[1,8,16,2048]{3,2,1,0:T(8,128)} %slice.169), channel_id=1, source_target_pairs={{8,0},{10,2},{12,4},{14,6},{0,8},{2,10},{4,12},{6,14},{9,1},{11,3}... | collective-permute-start | bytes 3145736 | tf_op jit(solution)/shard_map/ppermute | solution.py:19
  33.2 9.7 %slice-start = ((s8[8388608]{0:T(1024)(128)(4,1)}), s8[4194304]{0:T(1024)(128)(4,1)S(1)}, s32[]{:S(2)}) async-start(s8[8388608]{0:T(1024)(128)(4,1)} %bitcast.163), calls=%async_computation.2 | async-start | bytes 8388608
  33.2 9.7 %slice-start.1 = ((s8[8388608]{0:T(1024)(128)(4,1)}), s8[4194304]{0:T(1024)(128)(4,1)S(1)}, s32[]{:S(2)}) async-start(s8[8388608]{0:T(1024)(128)(4,1)} %bitcast.163), calls=%async_computation.3 | async-start | bytes 8388608
  52.6 10.9 %copy-start.4 = (f32[1,4,16,2048]{3,2,1,0:T(8,128)}, f32[1,4,16,2048]{3,2,1,0:T(8,128)S(1)}, u32[]{:S(2)}) copy-start(f32[1,4,16,2048]{3,2,1,0:T(8,128)S(1)} %collective-permute-done) | copy-start | bytes 1572868
  90.5 9.4 %copy-start = (f32[64,32,512]{2,1,0:T(8,128)S(1)}, f32[64,32,512]{2,1,0:T(8,128)}, u32[]{:S(2)}) copy-start(f32[64,32,512]{2,1,0:T(8,128)} %reshape_reshape.13) | copy-start | bytes 12582916
  108.8 8.8 %copy-start.1 = (f32[64,32,512]{2,1,0:T(8,128)S(1)}, f32[64,32,512]{2,1,0:T(8,128)}, u32[]{:S(2)}) copy-start(f32[64,32,512]{2,1,0:T(8,128)} %fusion.9) | copy-start | bytes 12582916
  117.6 4.0 %copy-start.2 = (f32[1,8,16,2048]{3,2,1,0:T(8,128)}, f32[1,8,16,2048]{3,2,1,0:T(8,128)S(1)}, u32[]{:S(2)}) copy-start(f32[1,8,16,2048]{3,2,1,0:T(8,128)S(1)} %collective-permute-done.1) | copy-start | bytes 3145732
  138.6 37.4 %collective-permute-start.2 = (f32[96,1024]{1,0:T(8,128)S(1)}, f32[96,1024]{1,0:T(8,128)S(1)}, u32[]{:S(2)}, u32[]{:S(2)}) collective-permute-start(f32[96,1024]{1,0:T(8,128)S(1)} %mul.1433), channel_id=1, source_target_pairs={{8,0},{10,2},{12,4},{14,6},{0,8},{2,10},{4,12},{6,14},{9,1},{11,3}... | collective-permute-start | bytes 1179656 | tf_op jit(solution)/shard_map/ppermute | solution.py:19
  141.1 53.1 %collective-permute-start.3 = (f32[96,1024]{1,0:T(8,128)S(1)}, f32[96,1024]{1,0:T(8,128)S(1)}, u32[]{:S(2)}, u32[]{:S(2)}) collective-permute-start(f32[96,1024]{1,0:T(8,128)S(1)} %mul.1433), channel_id=1, source_target_pairs={{10,0},{12,2},{14,4},{0,6},{2,8},{4,10},{6,12},{8,14},{11,1},{13,3... | collective-permute-start | bytes 1179656 | tf_op jit(solution)/shard_map/ppermute | solution.py:19
  143.7 50.8 %collective-permute-start.4 = (f32[96,1024]{1,0:T(8,128)S(1)}, f32[96,1024]{1,0:T(8,128)S(1)}, u32[]{:S(2)}, u32[]{:S(2)}) collective-permute-start(f32[96,1024]{1,0:T(8,128)S(1)} %mul.1433), channel_id=1, source_target_pairs={{12,0},{14,2},{0,4},{2,6},{4,8},{6,10},{8,12},{10,14},{13,1},{15,3... | collective-permute-start | bytes 1179656 | tf_op jit(solution)/shard_map/ppermute | solution.py:19
  143.7 51.0 %collective-permute-start.5 = (f32[96,1024]{1,0:T(8,128)S(1)}, f32[96,1024]{1,0:T(8,128)S(1)}, u32[]{:S(2)}, u32[]{:S(2)}) collective-permute-start(f32[96,1024]{1,0:T(8,128)S(1)} %mul.1433), channel_id=1, source_target_pairs={{14,0},{0,2},{2,4},{4,6},{6,8},{8,10},{10,12},{12,14},{15,1},{1,3}... | collective-permute-start | bytes 1179656 | tf_op jit(solution)/shard_map/ppermute | solution.py:19
  194.9 0.7 copy-start.11
  195.2 0.7 copy-start.10
  200.1 1.4 copy-start.9
  204.8 4.3 %copy-start.5 = (f32[1,4,16,2048]{3,2,1,0:T(8,128)S(1)}, f32[1,4,16,2048]{3,2,1,0:T(8,128)}, u32[]{:S(2)}) copy-start(f32[1,4,16,2048]{3,2,1,0:T(8,128)} %copy-done.4) | copy-start | bytes 1572868
  209.0 1.4 copy-start.3
  209.0 1.4 copy-start.6
  209.0 1.4 copy-start.7
  209.0 1.5 copy-start.8
  210.9 1.1 copy-start.12
